TPU v7x, 256 devices: a whole 4x4x8 slice. The times are simulated.
256 devices in a mesh: req: 32 (over y, z), head: 8 (over x, core).
Axes of the slice: x: 4, y: 4, z: 8, core: 2. Of those that a mesh axis runs over, the one named last changes fastest.
Arguments:
- tokens: bfloat16 [32768, 1024], P(('req', 'head')), may hold values from -6 to 6
- w_proj: bfloat16 [1024, 2048], P(None, 'head'), may hold values from -0.1875 to 0.1875
- w_out: bfloat16 [1024, 1024], replicated, may hold values from -0.1875 to 0.1875
- kv_cache: bfloat16 [32, 32, 3, 128, 2048], P('req', None, None, None, 'head'), may hold values from -6 to 6
- slot_request: int32 [64], P('req'), may hold values from 0 to 63, each once
- lengths: int32 [64], replicated, may hold values from 1 to 4096
- block_owner: int32 [2048, 1], P('req'), may hold values from 0 to 31; in each aligned block of 64 rows (0 to 63, 64 to 127, ...) at most 3 rows name the same one
Outputs:
- mixed: bfloat16 [32768, 1024], P(('req', 'head'))
Inputs may be any that keep to these rules, and one draw needn't show every extreme that they name: `block_owner`: within each aligned block of 64 rows no owner appears more than 3 times.
All inputs are finite; a program needn't handle non-finite values.
Results may differ from a plain program's by a relative error of at most 0.0088.
Values may be sent and summed in bfloat16 or wider, within the bound.
No kernel may reach another device: no remote copies, remote signals or barrier semaphores. Data moves between devices by JAX's collectives and lax.ppermute only.
A program may use at most 128 MiB of HBM per device.

v0:
```python
import functools

import jax
import jax.numpy as jnp
from jax import lax
from jax.experimental import pallas as pl
from jax.experimental.pallas import tpu as pltpu
from jax.sharding import PartitionSpec as P

DH = 64
CAND = 512
BLK = 128
MAXB = 32


def layer_norm(values):
    mean = jnp.mean(values, axis=-1, keepdims=True)
    square = jnp.mean(values * values, axis=-1, keepdims=True)
    return (values - mean) * lax.rsqrt(square - mean * mean + 1e-05)


def attention_kernel(index_ref, length_ref, query_ref, *refs, heads, group):
    pool_refs = refs[:group]
    out_ref, acc_ref = refs[group:]
    slot = pl.program_id(0)
    step = pl.program_id(1)
    length = length_ref[slot]

    @pl.when(step == 0)
    def _():
        acc_ref[...] = jnp.zeros_like(acc_ref)

    for i in range(group):
        block = step * group + i

        @pl.when(block * BLK < length)
        def _():
            kv = pool_refs[i][0]
            positions = block * BLK + lax.broadcasted_iota(jnp.int32, (1, BLK), 1)
            live = positions < length
            for h in range(heads):
                lanes = slice(h * 2 * DH, (h + 1) * 2 * DH)
                pair = kv[:, lanes]
                query = query_ref[:, lanes]
                half = lax.dot_general(
                    query, pair, (((1,), (1,)), ((), ())), preferred_element_type=jnp.float32
                ) * (0.5 / DH**0.5)
                weights = half + half * jnp.tanh(half)
                weights = jnp.where(live, weights, 0.0).astype(jnp.bfloat16)
                acc_ref[:, lanes] += jnp.dot(weights, pair, preferred_element_type=jnp.float32)

    @pl.when(step == pl.num_programs(1) - 1)
    def _():
        out_ref[...] = acc_ref[...].astype(out_ref.dtype)


def pool_spec(width, group, i):
    return pl.BlockSpec(
        (1, BLK, width), lambda s, g, idx, lens: (idx[s * MAXB + g * group + i], 0, 0)
    )


def attention(index, slot_lengths, query_pad, pool, group=8):
    rows, width = query_pad.shape
    slots = rows // CAND
    heads = width // (2 * DH)
    kernel = functools.partial(attention_kernel, heads=heads, group=group)
    grid_spec = pltpu.PrefetchScalarGridSpec(
        num_scalar_prefetch=2,
        grid=(slots, MAXB // group),
        in_specs=[pl.BlockSpec((CAND, width), lambda s, g, idx, lens: (s, 0))]
        + [pool_spec(width, group, i) for i in range(group)],
        out_specs=pl.BlockSpec((CAND, width), lambda s, g, idx, lens: (s, 0)),
        scratch_shapes=[pltpu.VMEM((CAND, width), jnp.float32)],
    )
    return pl.pallas_call(
        kernel,
        grid_spec=grid_spec,
        out_shape=jax.ShapeDtypeStruct((rows, width), jnp.bfloat16),
        compiler_params=pltpu.CompilerParams(dimension_semantics=("arbitrary", "arbitrary")),
    )(index, slot_lengths, query_pad, *([pool] * group))


def shards(tokens, w_proj, w_out, kv_cache, slot_request, lengths, block_owner):
    head_local = w_proj.shape[1] // (2 * DH)
    received = lax.all_to_all(kv_cache, "req", split_axis=1, concat_axis=0, tiled=True)
    most_slots = received.shape[2]
    pool = received.reshape(-1, BLK, received.shape[-1])
    pool_count = pool.shape[0]

    gathered = lax.all_gather(tokens, "head", axis=0, tiled=True)
    normed = layer_norm(gathered.astype(jnp.float32)).astype(jnp.bfloat16)
    row_count = normed.shape[0]
    slots = row_count // CAND
    proj = jax.nn.silu(jnp.dot(normed, w_proj, preferred_element_type=jnp.float32))
    proj = proj.reshape(row_count, head_local, 2, DH)
    gate_u = proj[:, :, 0].astype(jnp.bfloat16).reshape(row_count, head_local * DH)
    query = proj[:, :, 1].astype(jnp.bfloat16)
    query_pad = jnp.concatenate([query, jnp.zeros_like(query)], axis=2).reshape(
        row_count, head_local * 2 * DH
    )

    owner_count = lax.axis_size("req")
    owners = block_owner[:, 0]
    onehot = (owners[:, None] == jnp.arange(owner_count, dtype=jnp.int32)[None, :]).astype(
        jnp.int32
    )
    rank = jnp.sum((jnp.cumsum(onehot, axis=0) - onehot) * onehot, axis=1)
    index = jnp.clip(owners * most_slots + rank, 0, pool_count - 1).reshape(slots, MAXB)
    total_requests = lengths.shape[0]
    match = slot_request[:, None] == jnp.arange(total_requests, dtype=jnp.int32)[None, :]
    slot_lengths = jnp.sum(jnp.where(match, lengths[None, :], 0), axis=1).astype(jnp.int32)
    last_live = jnp.clip((slot_lengths - 1) // BLK, 0, MAXB - 1)
    blocks = jnp.minimum(jnp.arange(MAXB, dtype=jnp.int32)[None, :], last_live[:, None])
    index = jnp.take_along_axis(index, blocks, axis=1).reshape(-1).astype(jnp.int32)

    out = attention(index, slot_lengths, query_pad, pool)
    attn = out.reshape(row_count, head_local, 2, DH)[:, :, 1].reshape(row_count, head_local * DH)

    gate_rows = lax.all_to_all(gate_u, "head", split_axis=0, concat_axis=1, tiled=True)
    attn_rows = lax.all_to_all(attn, "head", split_axis=0, concat_axis=1, tiled=True)
    attn_rows = attn_rows.astype(jnp.float32)
    gate_rows = gate_rows.astype(jnp.float32)
    hidden = (layer_norm(attn_rows) * gate_rows).astype(jnp.bfloat16)
    return jnp.dot(hidden, w_out, preferred_element_type=jnp.float32).astype(jnp.bfloat16)


def solution(mesh):
    return jax.shard_map(
        shards,
        mesh=mesh,
        in_specs=(
            P(("req", "head"), None),
            P(None, "head"),
            P(),
            P("req", None, None, None, "head"),
            P("req"),
            P(),
            P("req", None),
        ),
        out_specs=P(("req", "head"), None),
        check_vma=False,
    )
```

profile of v0, /device:TPU:104, one launch (start us, length us, event | category | flops | bytes accessed | tf_op | source)
XLA Modules:
  0.0 223.1 jit_solution(5403251056844648247)
XLA Ops:
  6.5 0.0 copy-start
  6.5 0.0 copy-start.2
  6.5 0.0 copy-start.5
  6.5 0.0 copy-start.6
  6.5 10.5 %all-to-all-start = ((bf16[1,32,3,128,256]{4,3,2,0,1:T(8,128)(2,1)}), bf16[1,32,3,128,256]{4,3,2,0,1:T(8,128)(2,1)}, u32[]{:S(2)}, u32[]{:S(2)}) async-start(bf16[1,32,3,128,256]{4,3,2,0,1:T(8,128)(2,1)} %bitcast.44), calls=%async_computation | async-start | bytes 12582912 | tf_op jit(solution)/shard_map/all_to_all | solution.py:86
  17.1 0.0 copy-start.4
  17.1 0.0 all-gather.2.cloned.1.call-start
  17.1 0.7 all-gather.2.cloned.1.call-update
  17.8 0.0 copy-done.2
  17.9 0.1 mul.62
  17.9 0.0 copy-done.5
  17.9 0.0 copy-done.6
  17.9 0.2 fusion.12.length_ref
  18.1 0.0 copy-start.3
  18.2 0.1 fusion.15
  18.2 0.1 reshape.159
  18.3 0.1 min.53
  18.4 0.1 min.54
  18.5 0.1 min.50
  18.6 0.1 fusion.11
  18.6 0.1 reduce_window_sum.11
  18.7 0.2 select_reduce_fusion
  18.9 0.1 reduce_sum.58
  19.0 0.9 gather_fusion
  19.9 0.5 and_select_fusion.index_ref
  20.4 28.3 %all-gather.2.cloned.1.call-done = bf16[1024,1024]{1,0:T(8,128)(2,1)} async-done(((bf16[128,1024]{1,0:T(8,128)(2,1)}), bf16[1024,1024]{1,0:T(8,128)(2,1)}) %all-gather.2.cloned.1.call-update) | async-done | bytes 2097168 | tf_op jit(solution)/shard_map/all_gather | solution.py:91
  48.7 0.0 copy-start.1
  48.7 2.4 %convert_reduce_fusion = (f32[1024]{0:T(1024)S(1)}, f32[1024]{0:T(1024)S(1)}) fusion(bf16[1024,1024]{1,0:T(8,128)(2,1)} %all-gather.2.cloned.1.call-done), kind=kLoop, calls=%fused_computation.3 | loop fusion | flops 4192256 | bytes 2105344 | tf_op jit(solution)/shard_map/reduce_sum | solution.py:17
  51.2 0.0 copy-done.4
  51.2 0.0 copy-done.1
  51.2 1.3 multiply_convert_fusion
  52.5 0.0 copy-done.3
  52.5 0.4 copy.29
  52.9 0.5 concatenate.3
  53.5 0.9 copy.35
  54.4 102.6 %all-to-all-done = bf16[1,32,3,128,256]{4,3,2,0,1:T(8,128)(2,1)} async-done(((bf16[1,32,3,128,256]{4,3,2,0,1:T(8,128)(2,1)}), bf16[1,32,3,128,256]{4,3,2,0,1:T(8,128)(2,1)}, u32[]{:S(2)}, u32[]{:S(2)}) %all-to-all-start) | async-done | bytes 6291488 | tf_op jit(solution)/shard_map/all_to_all | solution.py:86
  157.0 33.1 %shard_map.73 = bf16[1024,256]{1,0:T(8,128)(2,1)} custom-call(s32[64]{0:T(128)} %and_select_fusion.index_ref, s32[2]{0:T(128)} %copy-done.3, bf16[1024,256]{1,0:T(8,128)(2,1)} %bitcast.45, bf16[96,128,256]{2,1,0:T(8,128)(2,1)} %bitcast.4.refs_0_.refs_1_.refs_2_.refs_3_.refs_4_.refs_5_.refs_6_.refs_7_, ...), custom_call_target="tpu_custom_call" | custom-call | tf_op jit(solution)/shard_map/pallas_call | solution.py:76
  190.1 1.2 copy.25
  191.5 0.7 copy.26
  192.2 4.3 %all-to-all-start.1 = ((bf16[8,128,128]{1,2,0:T(8,128)(2,1)}), bf16[8,128,128]{1,2,0:T(8,128)(2,1)S(1)}, u32[]{:S(2)}, u32[]{:S(2)}) async-start(bf16[8,128,128]{1,2,0:T(8,128)(2,1)} %copy.26), calls=%async_computation.1 | async-start | bytes 524288 | tf_op jit(solution)/shard_map/all_to_all | solution.py:121
  196.6 0.7 copy.28
  197.3 6.7 %all-to-all-done.1 = bf16[8,128,128]{1,2,0:T(8,128)(2,1)S(1)} async-done(((bf16[8,128,128]{1,2,0:T(8,128)(2,1)}), bf16[8,128,128]{1,2,0:T(8,128)(2,1)S(1)}, u32[]{:S(2)}, u32[]{:S(2)}) %all-to-all-start.1) | async-done | bytes 262176 | tf_op jit(solution)/shard_map/all_to_all | solution.py:121
  204.1 3.4 %all-to-all-start.2 = ((bf16[8,128,128]{1,2,0:T(8,128)(2,1)}), bf16[8,128,128]{1,2,0:T(8,128)(2,1)S(1)}, u32[]{:S(2)}, u32[]{:S(2)}) async-start(bf16[8,128,128]{1,2,0:T(8,128)(2,1)} %copy.28), calls=%async_computation.2 | async-start | bytes 524288 | tf_op jit(solution)/shard_map/all_to_all | solution.py:120
  207.5 0.2 convert_reduce_fusion.1
  207.6 7.3 %all-to-all-done.2 = bf16[8,128,128]{1,2,0:T(8,128)(2,1)S(1)} async-done(((bf16[8,128,128]{1,2,0:T(8,128)(2,1)}), bf16[8,128,128]{1,2,0:T(8,128)(2,1)S(1)}, u32[]{:S(2)}, u32[]{:S(2)}) %all-to-all-start.2) | async-done | bytes 262176 | tf_op jit(solution)/shard_map/all_to_all | solution.py:120
  214.9 0.1 fusion.9
  215.1 0.0 copy-done
  215.1 1.2 convolution_convert_fusion
  (10 shorter events, 0.2 us)
Async XLA Ops:
  6.5 208.5 %copy-start = (bf16[1024,1024]{1,0:T(8,128)(2,1)S(1)}, bf16[1024,1024]{1,0:T(8,128)(2,1)}, u32[]{:S(2)}) copy-start(bf16[1024,1024]{1,0:T(8,128)(2,1)} %param.9) | copy-start | bytes 6291460
  6.5 11.3 %copy-start.2 = (s32[64,1]{0,1:T(1,128)S(1)}, s32[64,1]{0,1:T(1,128)}, u32[]{:S(2)}) copy-start(s32[64,1]{0,1:T(1,128)} %param.13) | copy-start | bytes 772
  6.5 11.4 %copy-start.5 = (s32[64]{0:T(128)S(1)}, s32[64]{0:T(128)}, u32[]{:S(2)}) copy-start(s32[64]{0:T(128)} %param.12) | copy-start | bytes 772
  6.5 11.4 %copy-start.6 = (s32[2]{0:T(128)S(1)}, s32[2]{0:T(128)}, u32[]{:S(2)}) copy-start(s32[2]{0:T(128)} %param.11) | copy-start | bytes 28
  6.5 150.5 %all-to-all-start = ((bf16[1,32,3,128,256]{4,3,2,0,1:T(8,128)(2,1)}), bf16[1,32,3,128,256]{4,3,2,0,1:T(8,128)(2,1)}, u32[]{:S(2)}, u32[]{:S(2)}) async-start(bf16[1,32,3,128,256]{4,3,2,0,1:T(8,128)(2,1)} %bitcast.44), calls=%async_computation | async-start | bytes 12582912 | tf_op jit(solution)/shard_map/all_to_all | solution.py:86
  17.1 34.1 %copy-start.4 = (bf16[1024,256]{1,0:T(8,128)(2,1)S(1)}, bf16[1024,256]{1,0:T(8,128)(2,1)}, u32[]{:S(2)}) copy-start(bf16[1024,256]{1,0:T(8,128)(2,1)} %param.8) | copy-start | bytes 1572868
  17.1 31.7 %all-gather.2.cloned.1.call-start = ((), (), s32[]{:S(2)}) async-start(), calls=%async_computation.3 | async-start | bytes 2359296 | tf_op jit(solution)/shard_map/all_gather | solution.py:91
  18.1 34.3 %copy-start.3 = (s32[2]{0:T(128)}, s32[2]{0:T(128)S(1)}, u32[]{:S(2)}) copy-start(s32[2]{0:T(128)S(1)} %fusion.12.length_ref) | copy-start | bytes 28
  48.7 2.4 %copy-start.1 = (bf16[1024,1024]{1,0:T(8,128)(2,1)S(1)}, bf16[1024,1024]{1,0:T(8,128)(2,1)}, u32[]{:S(2)}) copy-start(bf16[1024,1024]{1,0:T(8,128)(2,1)} %all-gather.2.cloned.1.call-done) | copy-start | bytes 6291460
  192.2 11.8 %all-to-all-start.1 = ((bf16[8,128,128]{1,2,0:T(8,128)(2,1)}), bf16[8,128,128]{1,2,0:T(8,128)(2,1)S(1)}, u32[]{:S(2)}, u32[]{:S(2)}) async-start(bf16[8,128,128]{1,2,0:T(8,128)(2,1)} %copy.26), calls=%async_computation.1 | async-start | bytes 524288 | tf_op jit(solution)/shard_map/all_to_all | solution.py:121
  204.1 10.9 %all-to-all-start.2 = ((bf16[8,128,128]{1,2,0:T(8,128)(2,1)}), bf16[8,128,128]{1,2,0:T(8,128)(2,1)S(1)}, u32[]{:S(2)}, u32[]{:S(2)}) async-start(bf16[8,128,128]{1,2,0:T(8,128)(2,1)} %copy.28), calls=%async_computation.2 | async-start | bytes 524288 | tf_op jit(solution)/shard_map/all_to_all | solution.py:120
Sparse Core Ops, SparseCore 0:
  19.8 28.9 all-gather.1
where the time goes:
time: 224 us; the launch traced here: 223 us
  waiting for transfers between devices  146 us (65%)
  Pallas kernels  33.1 us (15%)
  starting transfers between devices  18.3 us (8%)
  between operations  13.6 us (6%)
  local copies, waits for them, and re-layouts  6.12 us (3%)
  other arithmetic  3.85 us (2%)
  matrix products  2.45 us (1%)
    all_to_all x1, waiting for transfers between devices, shards(): lax.all_to_all(kv_cache, 'req', split_axis=1, concat_axis=0, tiled=True)  103 us
    pallas_call x1, Pallas kernels, attention(): pl.pallas_call(kernel, grid_spec=grid_spec, out_shape=jax.ShapeDtypeStruc...  33.1 us
    all_gather x1, waiting for transfers between devices, shards(): gathered = lax.all_gather(tokens, 'head', axis=0, tiled=True)  28.3 us
    all_to_all x1, starting transfers between devices, shards(): lax.all_to_all(kv_cache, 'req', split_axis=1, concat_axis=0, tiled=True)  10.5 us
    all_to_all x1, waiting for transfers between devices, shards(): lax.all_to_all(gate_u, 'head', split_axis=0, concat_axis=1, tiled=True)  7.29 us
    all_to_all x1, waiting for transfers between devices, shards(): lax.all_to_all(attn, 'head', split_axis=0, concat_axis=1, tiled=True)  6.75 us
  transfers between devices with their start and end apart: 4, of which 4 were waited for; matrix products, arithmetic and copies ran while one was open for 4% of the time, Pallas kernels for 0%

commit v1 on v0

--- a/solution.py
+++ b/solution.py
@@ -30,24 +30,22 @@
     def _():
         acc_ref[...] = jnp.zeros_like(acc_ref)
 
-    for i in range(group):
-        block = step * group + i
+    span = group * BLK
 
-        @pl.when(block * BLK < length)
-        def _():
-            kv = pool_refs[i][0]
-            positions = block * BLK + lax.broadcasted_iota(jnp.int32, (1, BLK), 1)
-            live = positions < length
-            for h in range(heads):
-                lanes = slice(h * 2 * DH, (h + 1) * 2 * DH)
-                pair = kv[:, lanes]
-                query = query_ref[:, lanes]
-                half = lax.dot_general(
-                    query, pair, (((1,), (1,)), ((), ())), preferred_element_type=jnp.float32
-                ) * (0.5 / DH**0.5)
-                weights = half + half * jnp.tanh(half)
-                weights = jnp.where(live, weights, 0.0).astype(jnp.bfloat16)
-                acc_ref[:, lanes] += jnp.dot(weights, pair, preferred_element_type=jnp.float32)
+    @pl.when(step * span < length)
+    def _():
+        kv = jnp.concatenate([ref[0] for ref in pool_refs], axis=0)
+        positions = step * span + lax.broadcasted_iota(jnp.int32, (span, 1), 0)
+        kv = jnp.where(positions < length, kv, jnp.zeros_like(kv))
+        for h in range(heads):
+            lanes = slice(h * 2 * DH, (h + 1) * 2 * DH)
+            pair = kv[:, lanes]
+            query = query_ref[:, lanes]
+            half = lax.dot_general(
+                query, pair, (((1,), (1,)), ((), ())), preferred_element_type=jnp.float32
+            ) * (0.5 / DH**0.5)
+            weights = (half + half * jnp.tanh(half)).astype(jnp.bfloat16)
+            acc_ref[:, lanes] += jnp.dot(weights, pair, preferred_element_type=jnp.float32)
 
     @pl.when(step == pl.num_programs(1) - 1)
     def _():
@@ -117,10 +115,9 @@
     out = attention(index, slot_lengths, query_pad, pool)
     attn = out.reshape(row_count, head_local, 2, DH)[:, :, 1].reshape(row_count, head_local * DH)
 
-    gate_rows = lax.all_to_all(gate_u, "head", split_axis=0, concat_axis=1, tiled=True)
-    attn_rows = lax.all_to_all(attn, "head", split_axis=0, concat_axis=1, tiled=True)
-    attn_rows = attn_rows.astype(jnp.float32)
-    gate_rows = gate_rows.astype(jnp.float32)
+    moved = lax.all_to_all(jnp.stack([attn, gate_u]), "head", split_axis=1, concat_axis=2, tiled=True)
+    attn_rows = moved[0].astype(jnp.float32)
+    gate_rows = moved[1].astype(jnp.float32)
     hidden = (layer_norm(attn_rows) * gate_rows).astype(jnp.bfloat16)
     return jnp.dot(hidden, w_out, preferred_element_type=jnp.float32).astype(jnp.bfloat16)
 

time: 224 us -> 202 us (0.902)
  the two profiles are of different devices: /device:TPU:104 before, /device:TPU:32 now
where the time goes in v1:
time: 202 us
  waiting for transfers between devices  132 us (65%)
  Pallas kernels  16.7 us (8%)
  blocking collectives  14.5 us (7%)
  between operations  13.6 us (7%)
  starting transfers between devices  11.6 us (6%)
  local copies, waits for them, and re-layouts  6.22 us (3%)
  other arithmetic  5.05 us (2%)
  matrix products  2.44 us (1%)
    all_to_all x1, waiting for transfers between devices, shards(): lax.all_to_all(kv_cache, 'req', split_axis=1, concat_axis=0, tiled=True)  104 us
    all_gather x1, waiting for transfers between devices, shards(): gathered = lax.all_gather(tokens, 'head', axis=0, tiled=True)  28.1 us
    pallas_call x1, Pallas kernels, attention(): pl.pallas_call(kernel, grid_spec=grid_spec, out_shape=jax.ShapeDtypeStruc...  16.7 us
    all_to_all x1, blocking collectives, shards(): lax.all_to_all(jnp.stack([attn, gate_u]), 'head', split_axis=1, concat_ax...  14.5 us
    all_to_all x1, starting transfers between devices, shards(): lax.all_to_all(kv_cache, 'req', split_axis=1, concat_axis=0, tiled=True)  11.5 us
  transfers between devices with their start and end apart: 2, of which 2 were waited for; matrix products, arithmetic and copies ran while one was open for 4% of the time, Pallas kernels for 0%

profile of v1, /device:TPU:32, one launch (start us, length us, event | category | flops | bytes accessed | tf_op | source)
XLA Modules:
  0.0 202.4 jit_solution(1734861261364573175)
XLA Ops:
  6.5 0.0 copy-start
  6.5 0.0 copy-start.2
  6.5 0.0 copy-start.5
  6.5 0.0 copy-start.6
  6.5 11.5 %all-to-all-start = ((bf16[1,32,3,128,256]{4,3,2,0,1:T(8,128)(2,1)}), bf16[1,32,3,128,256]{4,3,2,0,1:T(8,128)(2,1)}, u32[]{:S(2)}, u32[]{:S(2)}) async-start(bf16[1,32,3,128,256]{4,3,2,0,1:T(8,128)(2,1)} %bitcast.32), calls=%async_computation | async-start | bytes 12582912 | tf_op jit(solution)/shard_map/all_to_all | solution.py:84
  18.1 0.0 copy-start.4
  18.1 0.0 all-gather.2.cloned.1.call-start
  18.2 0.7 all-gather.2.cloned.1.call-update
  18.8 0.0 copy-done.2
  18.9 0.1 mul.61
  19.0 0.0 copy-done.5
  19.0 0.0 copy-done.6
  19.0 0.2 fusion.13.length_ref
  19.1 0.0 copy-start.3
  19.2 0.1 fusion.16
  19.2 0.1 reshape.163
  19.3 0.1 min.53
  19.4 0.1 min.54
  19.5 0.1 min.50
  19.6 0.1 fusion.12
  19.6 0.1 reduce_window_sum.11
  19.7 0.2 select_reduce_fusion
  19.9 0.1 reduce_sum.58
  20.0 0.9 gather_fusion
  20.9 0.5 and_select_fusion.index_ref
  21.4 28.1 %all-gather.2.cloned.1.call-done = bf16[1024,1024]{1,0:T(8,128)(2,1)} async-done(((bf16[128,1024]{1,0:T(8,128)(2,1)}), bf16[1024,1024]{1,0:T(8,128)(2,1)}) %all-gather.2.cloned.1.call-update) | async-done | bytes 2097168 | tf_op jit(solution)/shard_map/all_gather | solution.py:89
  49.6 2.4 %convert_reduce_fusion = (f32[1024]{0:T(1024)S(1)}, f32[1024]{0:T(1024)S(1)}) fusion(bf16[1024,1024]{1,0:T(8,128)(2,1)} %all-gather.2.cloned.1.call-done), kind=kLoop, calls=%fused_computation.3 | loop fusion | flops 4192256 | bytes 2105344 | tf_op jit(solution)/shard_map/reduce_sum | solution.py:17
  52.0 0.0 copy-done.4
  52.0 0.0 copy-done.1
  52.0 1.3 multiply_convert_fusion
  53.3 0.0 copy-done.3
  53.3 0.4 copy.31
  53.7 0.5 concatenate.3
  54.3 0.9 copy.34
  55.2 103.6 %all-to-all-done = bf16[1,32,3,128,256]{4,3,2,0,1:T(8,128)(2,1)} async-done(((bf16[1,32,3,128,256]{4,3,2,0,1:T(8,128)(2,1)}), bf16[1,32,3,128,256]{4,3,2,0,1:T(8,128)(2,1)}, u32[]{:S(2)}, u32[]{:S(2)}) %all-to-all-start) | async-done | bytes 6291488 | tf_op jit(solution)/shard_map/all_to_all | solution.py:84
  158.8 16.7 %shard_map.73 = bf16[1024,256]{1,0:T(8,128)(2,1)} custom-call(s32[64]{0:T(128)} %and_select_fusion.index_ref, s32[2]{0:T(128)} %copy-done.3, bf16[1024,256]{1,0:T(8,128)(2,1)} %bitcast.35, bf16[96,128,256]{2,1,0:T(8,128)(2,1)} %bitcast.4.refs_0_.refs_1_.refs_2_.refs_3_.refs_4_.refs_5_.refs_6_.refs_7_, ...), custom_call_target="tpu_custom_call" | custom-call | tf_op jit(solution)/shard_map/pallas_call | solution.py:74
  175.4 1.2 copy.26
  176.7 0.1 pad_maximum_fusion
  176.8 0.4 copy.27
  177.2 14.5 %all_to_all.24 = bf16[2,1024,128]{2,0,1:T(2,128)(2,1)S(1)} all-to-all(bf16[2,1024,128]{2,0,1:T(2,128)(2,1)S(1)} %copy.27), channel_id=1, replica_groups=mesh['req'=32,'head'=8] {'head'}, dimensions={1} | all-to-all | bytes 1048576 | tf_op jit(solution)/shard_map/all_to_all | solution.py:118
  191.7 0.1 copy.28
  191.8 0.1 fusion.11
  191.9 0.1 slice_convert_fusion.1
  192.0 1.0 copy.29
  193.0 0.2 copy.30
  193.2 1.2 fusion.9
  194.4 0.0 copy-done
  194.4 1.2 convolution_convert_fusion
  (9 shorter events, 0.1 us)
Async XLA Ops:
  6.5 187.9 %copy-start = (bf16[1024,1024]{1,0:T(8,128)(2,1)S(1)}, bf16[1024,1024]{1,0:T(8,128)(2,1)}, u32[]{:S(2)}) copy-start(bf16[1024,1024]{1,0:T(8,128)(2,1)} %param.9) | copy-start | bytes 6291460
  6.5 12.3 %copy-start.2 = (s32[64,1]{0,1:T(1,128)S(1)}, s32[64,1]{0,1:T(1,128)}, u32[]{:S(2)}) copy-start(s32[64,1]{0,1:T(1,128)} %param.13) | copy-start | bytes 772
  6.5 12.4 %copy-start.5 = (s32[64]{0:T(128)S(1)}, s32[64]{0:T(128)}, u32[]{:S(2)}) copy-start(s32[64]{0:T(128)} %param.12) | copy-start | bytes 772
  6.5 12.4 %copy-start.6 = (s32[2]{0:T(128)S(1)}, s32[2]{0:T(128)}, u32[]{:S(2)}) copy-start(s32[2]{0:T(128)} %param.11) | copy-start | bytes 28
  6.5 152.2 %all-to-all-start = ((bf16[1,32,3,128,256]{4,3,2,0,1:T(8,128)(2,1)}), bf16[1,32,3,128,256]{4,3,2,0,1:T(8,128)(2,1)}, u32[]{:S(2)}, u32[]{:S(2)}) async-start(bf16[1,32,3,128,256]{4,3,2,0,1:T(8,128)(2,1)} %bitcast.32), calls=%async_computation | async-start | bytes 12582912 | tf_op jit(solution)/shard_map/all_to_all | solution.py:84
  18.1 33.9 %copy-start.4 = (bf16[1024,256]{1,0:T(8,128)(2,1)S(1)}, bf16[1024,256]{1,0:T(8,128)(2,1)}, u32[]{:S(2)}) copy-start(bf16[1024,256]{1,0:T(8,128)(2,1)} %param.8) | copy-start | bytes 1572868
  18.1 31.5 %all-gather.2.cloned.1.call-start = ((), (), s32[]{:S(2)}) async-start(), calls=%async_computation.2 | async-start | bytes 2359296 | tf_op jit(solution)/shard_map/all_gather | solution.py:89
  19.1 34.1 %copy-start.3 = (s32[2]{0:T(128)}, s32[2]{0:T(128)S(1)}, u32[]{:S(2)}) copy-start(s32[2]{0:T(128)S(1)} %fusion.13.length_ref) | copy-start | bytes 28
  49.6 2.4 %copy-start.1 = (bf16[1024,1024]{1,0:T(8,128)(2,1)S(1)}, bf16[1024,1024]{1,0:T(8,128)(2,1)}, u32[]{:S(2)}) copy-start(bf16[1024,1024]{1,0:T(8,128)(2,1)} %all-gather.2.cloned.1.call-done) | copy-start | bytes 6291460
Sparse Core Ops, SparseCore 0:
  20.8 28.7 all-gather.1

commit v2 on v1

--- a/solution.py
+++ b/solution.py
@@ -79,6 +79,24 @@
     )(index, slot_lengths, query_pad, *([pool] * group))
 
 
+def exchange(values, axis):
+    count = lax.axis_size(axis)
+    me = lax.axis_index(axis)
+    rows = values.shape[0] // count
+    blocks = values.reshape(count, rows, values.shape[1])
+    received = []
+    for shift in range(count):
+        piece = lax.dynamic_index_in_dim(blocks, (me + shift) % count, 0, keepdims=False)
+        if shift:
+            pairs = [(i, (i + shift) % count) for i in range(count)]
+            piece = lax.ppermute(piece, axis, perm=pairs)
+        received.append(piece)
+    stacked = jnp.stack(received)
+    sources = (me - jnp.arange(count, dtype=jnp.int32)) % count
+    ordered = jnp.take(stacked, sources, axis=0)
+    return jnp.transpose(ordered, (1, 0, 2)).reshape(rows, count * values.shape[1])
+
+
 def shards(tokens, w_proj, w_out, kv_cache, slot_request, lengths, block_owner):
     head_local = w_proj.shape[1] // (2 * DH)
     received = lax.all_to_all(kv_cache, "req", split_axis=1, concat_axis=0, tiled=True)
@@ -112,12 +130,13 @@
     blocks = jnp.minimum(jnp.arange(MAXB, dtype=jnp.int32)[None, :], last_live[:, None])
     index = jnp.take_along_axis(index, blocks, axis=1).reshape(-1).astype(jnp.int32)
 
+    gate_rows = exchange(gate_u, "head")
+    gate_rows, query_pad = lax.optimization_barrier((gate_rows, query_pad))
     out = attention(index, slot_lengths, query_pad, pool)
     attn = out.reshape(row_count, head_local, 2, DH)[:, :, 1].reshape(row_count, head_local * DH)
 
-    moved = lax.all_to_all(jnp.stack([attn, gate_u]), "head", split_axis=1, concat_axis=2, tiled=True)
-    attn_rows = moved[0].astype(jnp.float32)
-    gate_rows = moved[1].astype(jnp.float32)
+    attn_rows = exchange(attn, "head").astype(jnp.float32)
+    gate_rows = gate_rows.astype(jnp.float32)
     hidden = (layer_norm(attn_rows) * gate_rows).astype(jnp.bfloat16)
     return jnp.dot(hidden, w_out, preferred_element_type=jnp.float32).astype(jnp.bfloat16)
 

time: 202 us -> 198 us (0.980)
  the two profiles are of different devices: /device:TPU:32 before, /device:TPU:112 now
where the time goes in v2:
time: 198 us; the launch traced here: 194 us
  waiting for transfers between devices  126 us (64%)
  starting transfers between devices  27.4 us (14%)
  between operations  13.9 us (7%)
  Pallas kernels  11.2 us (6%)
  local copies, waits for them, and re-layouts  9.51 us (5%)
  other arithmetic  4.14 us (2%)
  matrix products  2.44 us (1%)
    all_to_all x1, waiting for transfers between devices, shards(): lax.all_to_all(kv_cache, 'req', split_axis=1, concat_axis=0, tiled=True)  92.1 us
    all_gather x1, waiting for transfers between devices, shards(): gathered = lax.all_gather(tokens, 'head', axis=0, tiled=True)  28.2 us
    ppermute x14, starting transfers between devices, exchange(): piece = lax.ppermute(piece, axis, perm=pairs)  17 us
    pallas_call x1, Pallas kernels, attention(): pl.pallas_call(kernel, grid_spec=grid_spec, out_shape=jax.ShapeDtypeStruc...  11.2 us
    all_to_all x1, starting transfers between devices, shards(): lax.all_to_all(kv_cache, 'req', split_axis=1, concat_axis=0, tiled=True)  10.4 us
    ppermute x14, waiting for transfers between devices, exchange(): piece = lax.ppermute(piece, axis, perm=pairs)  4.6 us
  transfers between devices with their start and end apart: 16, of which 5 were waited for; matrix products, arithmetic and copies ran while one was open for 6% of the time, Pallas kernels for 0%

profile of v2, /device:TPU:112, one launch (start us, length us, event | category | flops | bytes accessed | tf_op | source)
XLA Modules:
  0.0 194.2 jit_solution(7205273992242023479)
XLA Ops:
  6.5 10.4 %all-to-all-start = ((bf16[1,32,3,128,256]{4,3,2,0,1:T(8,128)(2,1)}), bf16[1,32,3,128,256]{4,3,2,0,1:T(8,128)(2,1)}, u32[]{:S(2)}, u32[]{:S(2)}) async-start(bf16[1,32,3,128,256]{4,3,2,0,1:T(8,128)(2,1)} %bitcast.85), calls=%async_computation | async-start | bytes 12582912 | tf_op jit(solution)/shard_map/all_to_all | solution.py:102
  17.0 0.7 all-gather.2.cloned.1.call-update
  17.9 0.2 fusion.14.length_ref
  18.7 0.2 select_reduce_fusion
  19.0 0.9 gather_fusion
  19.9 0.5 and_select_fusion.1.index_ref
  20.5 28.2 %all-gather.2.cloned.1.call-done = bf16[1024,1024]{1,0:T(8,128)(2,1)} async-done(((bf16[128,1024]{1,0:T(8,128)(2,1)}), bf16[1024,1024]{1,0:T(8,128)(2,1)}) %all-gather.2.cloned.1.call-update) | async-done | bytes 2097168 | tf_op jit(solution)/shard_map/all_gather | solution.py:107
  48.7 2.4 %convert_reduce_fusion = (f32[1024]{0:T(1024)S(1)}, f32[1024]{0:T(1024)S(1)}) fusion(bf16[1024,1024]{1,0:T(8,128)(2,1)} %all-gather.2.cloned.1.call-done), kind=kLoop, calls=%fused_computation.5 | loop fusion | flops 4192256 | bytes 2105344 | tf_op jit(solution)/shard_map/reduce_sum | solution.py:17
  51.1 1.3 multiply_convert_fusion
  52.5 0.4 copy.81
  52.9 0.5 concatenate.3
  53.4 0.9 copy.87
  54.3 0.6 constant_dynamic-slice_fusion.8
  55.1 0.1 copy.62
  55.2 0.1 copy.61
  55.3 0.1 copy.60
  55.5 0.1 copy.59
  55.6 0.1 copy.80
  55.7 0.3 collective-permute-start
  56.0 0.2 collective-permute-start.1
  56.2 1.8 collective-permute-start.2
  58.0 2.2 %collective-permute-start.3 = (bf16[128,128]{1,0:T(8,128)(2,1)S(1)}, bf16[128,128]{1,0:T(8,128)(2,1)S(1)}, u32[]{:S(2)}, u32[]{:S(2)}) collective-permute-start(bf16[128,128]{1,0:T(8,128)(2,1)S(1)} %bitcast.98), channel_id=1, source_target_pairs={{0,4},{1,5},{2,6},{3,7},{4,0},{5,1},{6,2},{7,3},{8,12},{9,13},{10,... | collective-permute-start | bytes 98312 | tf_op jit(solution)/shard_map/ppermute | solution.py:92
  60.2 1.6 collective-permute-start.4
  61.9 0.1 copy.64
  62.1 2.0 %collective-permute-start.5 = (bf16[128,128]{1,0:T(8,128)(2,1)S(1)}, bf16[128,128]{1,0:T(8,128)(2,1)S(1)}, u32[]{:S(2)}, u32[]{:S(2)}) collective-permute-start(bf16[128,128]{1,0:T(8,128)(2,1)S(1)} %bitcast.104), channel_id=1, source_target_pairs={{0,6},{1,7},{2,0},{3,1},{4,2},{5,3},{6,4},{7,5},{8,14},{9,15},{10,... | collective-permute-start | bytes 98312 | tf_op jit(solution)/shard_map/ppermute | solution.py:92
  64.2 2.2 %collective-permute-done.5 = bf16[128,128]{1,0:T(8,128)(2,1)S(1)} collective-permute-done((bf16[128,128]{1,0:T(8,128)(2,1)S(1)}, bf16[128,128]{1,0:T(8,128)(2,1)S(1)}, u32[]{:S(2)}, u32[]{:S(2)}) %collective-permute-start.5) | collective-permute-done | bytes 32800 | tf_op jit(solution)/shard_map/ppermute | solution.py:92
  66.5 0.6 gather_fusion.1
  67.2 0.2 copy.66
  67.4 92.1 %all-to-all-done = bf16[1,32,3,128,256]{4,3,2,0,1:T(8,128)(2,1)} async-done(((bf16[1,32,3,128,256]{4,3,2,0,1:T(8,128)(2,1)}), bf16[1,32,3,128,256]{4,3,2,0,1:T(8,128)(2,1)}, u32[]{:S(2)}, u32[]{:S(2)}) %all-to-all-start) | async-done | bytes 6291488 | tf_op jit(solution)/shard_map/all_to_all | solution.py:102
  159.4 11.2 %shard_map.73 = bf16[1024,256]{1,0:T(8,128)(2,1)} custom-call(s32[64]{0:T(128)} %and_select_fusion.1.index_ref, s32[2]{0:T(128)} %copy-done.3, bf16[1024,256]{1,0:T(8,128)(2,1)} %bitcast.88, bf16[96,128,256]{2,1,0:T(8,128)(2,1)} %bitcast.20.refs_0_.refs_1_.refs_2_.refs_3_.refs_4_.refs_5_.refs_6_.refs_7_, ...), custom_call_target="tpu_custom_call" | custom-call | tf_op jit(solution)/shard_map/pallas_call | solution.py:74
  170.7 1.2 copy.69
  172.0 0.6 constant_dynamic-slice_fusion
  172.7 0.1 copy.74
  172.9 0.1 copy.73
  173.0 0.1 copy.72
  173.1 0.1 copy.71
  173.2 0.1 copy.82
  173.4 1.6 collective-permute-start.8
  175.0 2.0 %collective-permute-start.9 = (bf16[128,128]{1,0:T(8,128)(2,1)S(1)}, bf16[128,128]{1,0:T(8,128)(2,1)S(1)}, u32[]{:S(2)}, u32[]{:S(2)}) collective-permute-start(bf16[128,128]{1,0:T(8,128)(2,1)S(1)} %bitcast.101), channel_id=1, source_target_pairs={{0,3},{1,4},{2,5},{3,6},{4,7},{5,0},{6,1},{7,2},{8,11},{9,12},{10,... | collective-permute-start | bytes 98312 | tf_op jit(solution)/shard_map/ppermute | solution.py:92
  177.0 2.0 %collective-permute-start.10 = (bf16[128,128]{1,0:T(8,128)(2,1)S(1)}, bf16[128,128]{1,0:T(8,128)(2,1)S(1)}, u32[]{:S(2)}, u32[]{:S(2)}) collective-permute-start(bf16[128,128]{1,0:T(8,128)(2,1)S(1)} %bitcast.99), channel_id=1, source_target_pairs={{0,4},{1,5},{2,6},{3,7},{4,0},{5,1},{6,2},{7,3},{8,12},{9,13},{10,... | collective-permute-start | bytes 98312 | tf_op jit(solution)/shard_map/ppermute | solution.py:92
  179.0 1.6 collective-permute-start.11
  180.8 0.1 copy.76
  180.9 1.5 collective-permute-start.12
  182.6 2.3 %collective-permute-done.12 = bf16[128,128]{1,0:T(8,128)(2,1)S(1)} collective-permute-done((bf16[128,128]{1,0:T(8,128)(2,1)S(1)}, bf16[128,128]{1,0:T(8,128)(2,1)S(1)}, u32[]{:S(2)}, u32[]{:S(2)}) %collective-permute-start.12) | collective-permute-done | bytes 32800 | tf_op jit(solution)/shard_map/ppermute | solution.py:92
  184.9 0.6 gather_fusion.2
  185.5 0.2 convert_reduce_fusion.1
  185.9 0.2 copy.78
  186.2 1.2 convolution_convert_fusion
  (75 shorter events, 2.1 us)
Async XLA Ops:
  6.5 179.7 %copy-start = (bf16[1024,1024]{1,0:T(8,128)(2,1)S(1)}, bf16[1024,1024]{1,0:T(8,128)(2,1)}, u32[]{:S(2)}) copy-start(bf16[1024,1024]{1,0:T(8,128)(2,1)} %param.11) | copy-start | bytes 6291460
  6.5 11.3 %copy-start.2 = (s32[64,1]{0,1:T(1,128)S(1)}, s32[64,1]{0,1:T(1,128)}, u32[]{:S(2)}) copy-start(s32[64,1]{0,1:T(1,128)} %param.15) | copy-start | bytes 772
  6.5 11.4 %copy-start.5 = (s32[64]{0:T(128)S(1)}, s32[64]{0:T(128)}, u32[]{:S(2)}) copy-start(s32[64]{0:T(128)} %param.14) | copy-start | bytes 772
  6.5 11.4 %copy-start.6 = (s32[2]{0:T(128)S(1)}, s32[2]{0:T(128)}, u32[]{:S(2)}) copy-start(s32[2]{0:T(128)} %param.13) | copy-start | bytes 28
  6.5 152.9 %all-to-all-start = ((bf16[1,32,3,128,256]{4,3,2,0,1:T(8,128)(2,1)}), bf16[1,32,3,128,256]{4,3,2,0,1:T(8,128)(2,1)}, u32[]{:S(2)}, u32[]{:S(2)}) async-start(bf16[1,32,3,128,256]{4,3,2,0,1:T(8,128)(2,1)} %bitcast.85), calls=%async_computation | async-start | bytes 12582912 | tf_op jit(solution)/shard_map/all_to_all | solution.py:102
  17.0 34.1 %copy-start.4 = (bf16[1024,256]{1,0:T(8,128)(2,1)S(1)}, bf16[1024,256]{1,0:T(8,128)(2,1)}, u32[]{:S(2)}) copy-start(bf16[1024,256]{1,0:T(8,128)(2,1)} %param.10) | copy-start | bytes 1572868
  17.0 31.7 %all-gather.2.cloned.1.call-start = ((), (), s32[]{:S(2)}) async-start(), calls=%async_computation.1 | async-start | bytes 2359296 | tf_op jit(solution)/shard_map/all_gather | solution.py:107
  18.1 34.2 %copy-start.3 = (s32[2]{0:T(128)}, s32[2]{0:T(128)S(1)}, u32[]{:S(2)}) copy-start(s32[2]{0:T(128)S(1)} %fusion.14.length_ref) | copy-start | bytes 28
  48.7 2.4 %copy-start.1 = (bf16[1024,1024]{1,0:T(8,128)(2,1)S(1)}, bf16[1024,1024]{1,0:T(8,128)(2,1)}, u32[]{:S(2)}) copy-start(bf16[1024,1024]{1,0:T(8,128)(2,1)} %all-gather.2.cloned.1.call-done) | copy-start | bytes 6291460
  55.7 6.3 %collective-permute-start = (bf16[128,128]{1,0:T(8,128)(2,1)S(1)}, bf16[128,128]{1,0:T(8,128)(2,1)S(1)}, u32[]{:S(2)}, u32[]{:S(2)}) collective-permute-start(bf16[128,128]{1,0:T(8,128)(2,1)S(1)} %bitcast.108), channel_id=1, source_target_pairs={{0,1},{1,2},{2,3},{3,4},{4,5},{5,6},{6,7},{7,0},{8,9},{9,10},{10,1... | collective-permute-start | bytes 98312 | tf_op jit(solution)/shard_map/ppermute | solution.py:92
  56.0 8.1 %collective-permute-start.1 = (bf16[128,128]{1,0:T(8,128)(2,1)S(1)}, bf16[128,128]{1,0:T(8,128)(2,1)S(1)}, u32[]{:S(2)}, u32[]{:S(2)}) collective-permute-start(bf16[128,128]{1,0:T(8,128)(2,1)S(1)} %bitcast.106), channel_id=1, source_target_pairs={{0,2},{1,3},{2,4},{3,5},{4,6},{5,7},{6,0},{7,1},{8,10},{9,11},{10,... | collective-permute-start | bytes 98312 | tf_op jit(solution)/shard_map/ppermute | solution.py:92
  56.2 8.0 %collective-permute-start.2 = (bf16[128,128]{1,0:T(8,128)(2,1)S(1)}, bf16[128,128]{1,0:T(8,128)(2,1)S(1)}, u32[]{:S(2)}, u32[]{:S(2)}) collective-permute-start(bf16[128,128]{1,0:T(8,128)(2,1)S(1)} %bitcast.100), channel_id=1, source_target_pairs={{0,3},{1,4},{2,5},{3,6},{4,7},{5,0},{6,1},{7,2},{8,11},{9,12},{10,... | collective-permute-start | bytes 98312 | tf_op jit(solution)/shard_map/ppermute | solution.py:92
  58.0 6.2 %collective-permute-start.3 = (bf16[128,128]{1,0:T(8,128)(2,1)S(1)}, bf16[128,128]{1,0:T(8,128)(2,1)S(1)}, u32[]{:S(2)}, u32[]{:S(2)}) collective-permute-start(bf16[128,128]{1,0:T(8,128)(2,1)S(1)} %bitcast.98), channel_id=1, source_target_pairs={{0,4},{1,5},{2,6},{3,7},{4,0},{5,1},{6,2},{7,3},{8,12},{9,13},{10,... | collective-permute-start | bytes 98312 | tf_op jit(solution)/shard_map/ppermute | solution.py:92
  60.2 4.0 %collective-permute-start.4 = (bf16[128,128]{1,0:T(8,128)(2,1)S(1)}, bf16[128,128]{1,0:T(8,128)(2,1)S(1)}, u32[]{:S(2)}, u32[]{:S(2)}) collective-permute-start(bf16[128,128]{1,0:T(8,128)(2,1)S(1)} %bitcast.96), channel_id=1, source_target_pairs={{0,5},{1,6},{2,7},{3,0},{4,1},{5,2},{6,3},{7,4},{8,13},{9,14},{10,... | collective-permute-start | bytes 98312 | tf_op jit(solution)/shard_map/ppermute | solution.py:92
  62.1 4.4 %collective-permute-start.5 = (bf16[128,128]{1,0:T(8,128)(2,1)S(1)}, bf16[128,128]{1,0:T(8,128)(2,1)S(1)}, u32[]{:S(2)}, u32[]{:S(2)}) collective-permute-start(bf16[128,128]{1,0:T(8,128)(2,1)S(1)} %bitcast.104), channel_id=1, source_target_pairs={{0,6},{1,7},{2,0},{3,1},{4,2},{5,3},{6,4},{7,5},{8,14},{9,15},{10,... | collective-permute-start | bytes 98312 | tf_op jit(solution)/shard_map/ppermute | solution.py:92
  64.1 2.3 %collective-permute-start.6 = (bf16[128,128]{1,0:T(8,128)(2,1)S(1)}, bf16[128,128]{1,0:T(8,128)(2,1)S(1)}, u32[]{:S(2)}, u32[]{:S(2)}) collective-permute-start(bf16[128,128]{1,0:T(8,128)(2,1)S(1)} %bitcast.102), channel_id=1, source_target_pairs={{0,7},{1,0},{2,1},{3,2},{4,3},{5,4},{6,5},{7,6},{8,15},{9,8},{10,9... | collective-permute-start | bytes 98312 | tf_op jit(solution)/shard_map/ppermute | solution.py:92
  173.4 7.5 %collective-permute-start.7 = (bf16[128,128]{1,0:T(8,128)(2,1)S(1)}, bf16[128,128]{1,0:T(8,128)(2,1)S(1)}, u32[]{:S(2)}, u32[]{:S(2)}) collective-permute-start(bf16[128,128]{1,0:T(8,128)(2,1)S(1)} %bitcast.109), channel_id=1, source_target_pairs={{0,1},{1,2},{2,3},{3,4},{4,5},{5,6},{6,7},{7,0},{8,9},{9,10},{10,1... | collective-permute-start | bytes 98312 | tf_op jit(solution)/shard_map/ppermute | solution.py:92
  173.4 9.1 %collective-permute-start.8 = (bf16[128,128]{1,0:T(8,128)(2,1)S(1)}, bf16[128,128]{1,0:T(8,128)(2,1)S(1)}, u32[]{:S(2)}, u32[]{:S(2)}) collective-permute-start(bf16[128,128]{1,0:T(8,128)(2,1)S(1)} %bitcast.107), channel_id=1, source_target_pairs={{0,2},{1,3},{2,4},{3,5},{4,6},{5,7},{6,0},{7,1},{8,10},{9,11},{10,... | collective-permute-start | bytes 98312 | tf_op jit(solution)/shard_map/ppermute | solution.py:92
  175.0 7.5 %collective-permute-start.9 = (bf16[128,128]{1,0:T(8,128)(2,1)S(1)}, bf16[128,128]{1,0:T(8,128)(2,1)S(1)}, u32[]{:S(2)}, u32[]{:S(2)}) collective-permute-start(bf16[128,128]{1,0:T(8,128)(2,1)S(1)} %bitcast.101), channel_id=1, source_target_pairs={{0,3},{1,4},{2,5},{3,6},{4,7},{5,0},{6,1},{7,2},{8,11},{9,12},{10,... | collective-permute-start | bytes 98312 | tf_op jit(solution)/shard_map/ppermute | solution.py:92
  177.0 5.6 %collective-permute-start.10 = (bf16[128,128]{1,0:T(8,128)(2,1)S(1)}, bf16[128,128]{1,0:T(8,128)(2,1)S(1)}, u32[]{:S(2)}, u32[]{:S(2)}) collective-permute-start(bf16[128,128]{1,0:T(8,128)(2,1)S(1)} %bitcast.99), channel_id=1, source_target_pairs={{0,4},{1,5},{2,6},{3,7},{4,0},{5,1},{6,2},{7,3},{8,12},{9,13},{10,... | collective-permute-start | bytes 98312 | tf_op jit(solution)/shard_map/ppermute | solution.py:92
  179.0 3.6 %collective-permute-start.11 = (bf16[128,128]{1,0:T(8,128)(2,1)S(1)}, bf16[128,128]{1,0:T(8,128)(2,1)S(1)}, u32[]{:S(2)}, u32[]{:S(2)}) collective-permute-start(bf16[128,128]{1,0:T(8,128)(2,1)S(1)} %bitcast.97), channel_id=1, source_target_pairs={{0,5},{1,6},{2,7},{3,0},{4,1},{5,2},{6,3},{7,4},{8,13},{9,14},{10,... | collective-permute-start | bytes 98312 | tf_op jit(solution)/shard_map/ppermute | solution.py:92
  180.9 4.0 %collective-permute-start.12 = (bf16[128,128]{1,0:T(8,128)(2,1)S(1)}, bf16[128,128]{1,0:T(8,128)(2,1)S(1)}, u32[]{:S(2)}, u32[]{:S(2)}) collective-permute-start(bf16[128,128]{1,0:T(8,128)(2,1)S(1)} %bitcast.105), channel_id=1, source_target_pairs={{0,6},{1,7},{2,0},{3,1},{4,2},{5,3},{6,4},{7,5},{8,14},{9,15},{10,... | collective-permute-start | bytes 98312 | tf_op jit(solution)/shard_map/ppermute | solution.py:92
  182.5 2.5 %collective-permute-start.13 = (bf16[128,128]{1,0:T(8,128)(2,1)S(1)}, bf16[128,128]{1,0:T(8,128)(2,1)S(1)}, u32[]{:S(2)}, u32[]{:S(2)}) collective-permute-start(bf16[128,128]{1,0:T(8,128)(2,1)S(1)} %bitcast.103), channel_id=1, source_target_pairs={{0,7},{1,0},{2,1},{3,2},{4,3},{5,4},{6,5},{7,6},{8,15},{9,8},{10,9... | collective-permute-start | bytes 98312 | tf_op jit(solution)/shard_map/ppermute | solution.py:92
Sparse Core Ops, SparseCore 0:
  19.7 28.9 all-gather.1

commit v3 on v2

--- a/solution.py
+++ b/solution.py
@@ -79,22 +79,35 @@
     )(index, slot_lengths, query_pad, *([pool] * group))
 
 
-def exchange(values, axis):
+def exchange(values, axis, cores=2):
     count = lax.axis_size(axis)
+    chips = count // cores
     me = lax.axis_index(axis)
+    my_chip = me // cores
+    my_core = me % cores
     rows = values.shape[0] // count
-    blocks = values.reshape(count, rows, values.shape[1])
+    width = values.shape[1]
+    blocks = values.reshape(chips, cores, rows, width)
+    keep = lax.dynamic_index_in_dim(blocks, my_core, 1, keepdims=False)
+    other = lax.dynamic_index_in_dim(blocks, 1 - my_core, 1, keepdims=False)
+    swapped = lax.ppermute(other, axis, perm=[(i, i ^ 1) for i in range(count)])
+    both = jnp.stack([keep, swapped], axis=1)
+    by_source = jnp.take(both, jnp.stack([my_core, 1 - my_core]), axis=1)
     received = []
-    for shift in range(count):
-        piece = lax.dynamic_index_in_dim(blocks, (me + shift) % count, 0, keepdims=False)
+    for shift in range(chips):
+        piece = lax.dynamic_index_in_dim(by_source, (my_chip + shift) % chips, 0, keepdims=False)
         if shift:
-            pairs = [(i, (i + shift) % count) for i in range(count)]
+            pairs = [
+                (c * cores + k, ((c + shift) % chips) * cores + k)
+                for c in range(chips)
+                for k in range(cores)
+            ]
             piece = lax.ppermute(piece, axis, perm=pairs)
         received.append(piece)
     stacked = jnp.stack(received)
-    sources = (me - jnp.arange(count, dtype=jnp.int32)) % count
+    sources = (my_chip - jnp.arange(chips, dtype=jnp.int32)) % chips
     ordered = jnp.take(stacked, sources, axis=0)
-    return jnp.transpose(ordered, (1, 0, 2)).reshape(rows, count * values.shape[1])
+    return jnp.transpose(ordered, (2, 0, 1, 3)).reshape(rows, count * width)
 
 
 def shards(tokens, w_proj, w_out, kv_cache, slot_request, lengths, block_owner):

time: 198 us -> 200 us (1.010); the launches traced: 194 us -> 199 us
  starting transfers between devices: 27.4 us -> 19.1 us
  waiting for transfers between devices: 126 us -> 134 us
  Pallas kernels: 11.2 us -> 16 us
    ppermute x14 -> x6, starting transfers between devices: 17 us -> 8.23 us  [exchange(): piece = lax.ppermute(piece, axis, perm=pairs)]
    pallas_call x1, Pallas kernels: 11.2 us -> 16 us  [attention(): pl.pallas_call(kernel, grid_spec=grid_spec, out_shape=jax.ShapeDtypeStruc...]
    ppermute x14 -> x6, waiting for transfers between devices: 4.6 us -> 8.03 us  [exchange(): piece = lax.ppermute(piece, axis, perm=pairs)]
    all_to_all x1, waiting for transfers between devices: 92.1 us -> 94.6 us  [shards(): lax.all_to_all(kv_cache, 'req', split_axis=1, concat_axis=0, tiled=True)]
    ppermute x0 -> x2, waiting for transfers between devices: none -> 2.01 us  [exchange(): swapped = lax.ppermute(other, axis, perm=[(i, i ^ 1) for i in range(count)])]
  transfers between devices with their start and end apart: 16 -> 10, of which waited for: 5 -> 9; matrix products, arithmetic and copies ran while one was open for 6% -> 6% of each run, Pallas kernels for 0% -> 0%
where the time goes in v3:
time: 200 us; the launch traced here: 199 us
  waiting for transfers between devices  134 us (67%)
  starting transfers between devices  19.1 us (10%)
  Pallas kernels  16 us (8%)
  between operations  13.8 us (7%)
  local copies, waits for them, and re-layouts  9.43 us (5%)
  other arithmetic  4.54 us (2%)
  matrix products  2.43 us (1%)
    all_to_all x1, waiting for transfers between devices, shards(): lax.all_to_all(kv_cache, 'req', split_axis=1, concat_axis=0, tiled=True)  94.6 us
    all_gather x1, waiting for transfers between devices, shards(): gathered = lax.all_gather(tokens, 'head', axis=0, tiled=True)  28.2 us
    pallas_call x1, Pallas kernels, attention(): pl.pallas_call(kernel, grid_spec=grid_spec, out_shape=jax.ShapeDtypeStruc...  16 us
    all_to_all x1, starting transfers between devices, shards(): lax.all_to_all(kv_cache, 'req', split_axis=1, concat_axis=0, tiled=True)  10.4 us
    ppermute x6, starting transfers between devices, exchange(): piece = lax.ppermute(piece, axis, perm=pairs)  8.23 us
    ppermute x6, waiting for transfers between devices, exchange(): piece = lax.ppermute(piece, axis, perm=pairs)  8.03 us
  transfers between devices with their start and end apart: 10, of which 9 were waited for; matrix products, arithmetic and copies ran while one was open for 6% of the time, Pallas kernels for 0%

profile of v3, /device:TPU:112, one launch (start us, length us, event | category | flops | bytes accessed | tf_op | source)
XLA Modules:
  0.0 198.9 jit_solution(8958745880230434)
XLA Ops:
  6.5 10.4 %all-to-all-start = ((bf16[1,32,3,128,256]{4,3,2,0,1:T(8,128)(2,1)}), bf16[1,32,3,128,256]{4,3,2,0,1:T(8,128)(2,1)}, u32[]{:S(2)}, u32[]{:S(2)}) async-start(bf16[1,32,3,128,256]{4,3,2,0,1:T(8,128)(2,1)} %bitcast.72), calls=%async_computation | async-start | bytes 12582912 | tf_op jit(solution)/shard_map/all_to_all | solution.py:115
  17.0 0.7 all-gather.2.cloned.1.call-update
  17.9 0.2 fusion.14.length_ref
  18.5 0.1 reduce_window_sum.11
  18.6 0.2 select_reduce_fusion
  18.9 0.9 gather_fusion
  19.9 0.5 and_select_fusion.1.index_ref
  20.4 28.2 %all-gather.2.cloned.1.call-done = bf16[1024,1024]{1,0:T(8,128)(2,1)} async-done(((bf16[128,1024]{1,0:T(8,128)(2,1)}), bf16[1024,1024]{1,0:T(8,128)(2,1)}) %all-gather.2.cloned.1.call-update) | async-done | bytes 2097168 | tf_op jit(solution)/shard_map/all_gather | solution.py:120
  48.7 2.4 %convert_reduce_fusion = (f32[1024]{0:T(1024)S(1)}, f32[1024]{0:T(1024)S(1)}) fusion(bf16[1024,1024]{1,0:T(8,128)(2,1)} %all-gather.2.cloned.1.call-done), kind=kLoop, calls=%fused_computation.7 | loop fusion | flops 4192256 | bytes 2105344 | tf_op jit(solution)/shard_map/reduce_sum | solution.py:17
  51.1 1.3 multiply_convert_fusion
  52.4 0.2 convert_element_type.44
  52.6 0.5 constant_dynamic-slice_fusion.5
  53.2 0.2 copy.40
  53.3 0.3 collective-permute-start
  53.8 0.2 copy.51
  53.9 0.8 collective-permute-done
  54.8 0.6 gather_fusion.1
  55.4 0.1 select_bitcast_fusion.2
  55.5 1.5 collective-permute-start.3
  57.0 0.9 collective-permute-start.2
  57.9 1.2 collective-permute-start.1
  59.1 0.4 copy.52
  59.5 0.5 concatenate.3
  60.0 0.9 copy.56
  60.9 2.5 %collective-permute-done.2 = bf16[2,128,128]{2,1,0:T(8,128)(2,1)S(1)} collective-permute-done((bf16[2,128,128]{2,1,0:T(8,128)(2,1)S(1)}, bf16[2,128,128]{2,1,0:T(8,128)(2,1)S(1)}, u32[]{:S(2)}, u32[]{:S(2)}) %collective-permute-start.2) | collective-permute-done | bytes 65568 | tf_op jit(solution)/shard_map/ppermute | solution.py:105
  63.4 0.4 collective-permute-done.1
  63.9 0.6 gather_fusion.2
  64.6 0.2 copy.42
  64.8 94.6 %all-to-all-done = bf16[1,32,3,128,256]{4,3,2,0,1:T(8,128)(2,1)} async-done(((bf16[1,32,3,128,256]{4,3,2,0,1:T(8,128)(2,1)}), bf16[1,32,3,128,256]{4,3,2,0,1:T(8,128)(2,1)}, u32[]{:S(2)}, u32[]{:S(2)}) %all-to-all-start) | async-done | bytes 6291488 | tf_op jit(solution)/shard_map/all_to_all | solution.py:115
  159.4 16.0 %shard_map.73 = bf16[1024,256]{1,0:T(8,128)(2,1)} custom-call(s32[64]{0:T(128)} %and_select_fusion.1.index_ref, s32[2]{0:T(128)} %copy-done.3, bf16[1024,256]{1,0:T(8,128)(2,1)} %bitcast.73, bf16[96,128,256]{2,1,0:T(8,128)(2,1)} %bitcast.18.refs_0_.refs_1_.refs_2_.refs_3_.refs_4_.refs_5_.refs_6_.refs_7_, ...), custom_call_target="tpu_custom_call" | custom-call | tf_op jit(solution)/shard_map/pallas_call | solution.py:74
  175.4 1.2 copy.45
  176.7 0.2 reshape_reshape_squeeze.3
  176.8 0.5 constant_dynamic-slice_fusion.2
  177.4 0.2 copy.47
  177.6 0.2 copy.53
  177.8 1.2 collective-permute-done.4
  179.0 0.6 gather_fusion.3
  179.8 3.0 %collective-permute-start.7 = (bf16[2,128,128]{2,1,0:T(8,128)(2,1)S(1)}, bf16[2,128,128]{2,1,0:T(8,128)(2,1)S(1)}, u32[]{:S(2)}, u32[]{:S(2)}) collective-permute-start(bf16[2,128,128]{2,1,0:T(8,128)(2,1)S(1)} %get-tuple-element.20), channel_id=1, source_target_pairs={{0,6},{1,7},{2,0},{3,1},{4,2},{5,3},{6,4},{7,5},{8,14},{9,15},{10,... | collective-permute-start | bytes 196616 | tf_op jit(solution)/shard_map/ppermute | solution.py:105
  182.8 0.8 collective-permute-start.6
  183.6 0.9 collective-permute-start.5
  184.5 1.5 collective-permute-done.7
  186.0 2.9 %collective-permute-done.6 = bf16[2,128,128]{2,1,0:T(8,128)(2,1)S(1)} collective-permute-done((bf16[2,128,128]{2,1,0:T(8,128)(2,1)S(1)}, bf16[2,128,128]{2,1,0:T(8,128)(2,1)S(1)}, u32[]{:S(2)}, u32[]{:S(2)}) %collective-permute-start.6) | collective-permute-done | bytes 65568 | tf_op jit(solution)/shard_map/ppermute | solution.py:105
  188.9 0.7 collective-permute-done.5
  189.6 0.6 gather_fusion.4
  190.2 0.2 convert_reduce_fusion.1
  190.4 0.1 convert_bitcast_fusion
  190.5 0.2 copy.49
  190.9 1.2 convolution_convert_fusion
  (47 shorter events, 1.5 us)
Async XLA Ops:
  6.5 184.3 %copy-start = (bf16[1024,1024]{1,0:T(8,128)(2,1)S(1)}, bf16[1024,1024]{1,0:T(8,128)(2,1)}, u32[]{:S(2)}) copy-start(bf16[1024,1024]{1,0:T(8,128)(2,1)} %param.13) | copy-start | bytes 6291460
  6.5 11.2 %copy-start.2 = (s32[64,1]{0,1:T(1,128)S(1)}, s32[64,1]{0,1:T(1,128)}, u32[]{:S(2)}) copy-start(s32[64,1]{0,1:T(1,128)} %param.17) | copy-start | bytes 772
  6.5 11.3 %copy-start.5 = (s32[64]{0:T(128)S(1)}, s32[64]{0:T(128)}, u32[]{:S(2)}) copy-start(s32[64]{0:T(128)} %param.16) | copy-start | bytes 772
  6.5 11.3 %copy-start.6 = (s32[2]{0:T(128)S(1)}, s32[2]{0:T(128)}, u32[]{:S(2)}) copy-start(s32[2]{0:T(128)} %param.15) | copy-start | bytes 28
  6.5 152.9 %all-to-all-start = ((bf16[1,32,3,128,256]{4,3,2,0,1:T(8,128)(2,1)}), bf16[1,32,3,128,256]{4,3,2,0,1:T(8,128)(2,1)}, u32[]{:S(2)}, u32[]{:S(2)}) async-start(bf16[1,32,3,128,256]{4,3,2,0,1:T(8,128)(2,1)} %bitcast.72), calls=%async_computation | async-start | bytes 12582912 | tf_op jit(solution)/shard_map/all_to_all | solution.py:115
  17.0 34.1 %copy-start.4 = (bf16[1024,256]{1,0:T(8,128)(2,1)S(1)}, bf16[1024,256]{1,0:T(8,128)(2,1)}, u32[]{:S(2)}) copy-start(bf16[1024,256]{1,0:T(8,128)(2,1)} %param.12) | copy-start | bytes 1572868
  17.0 31.7 %all-gather.2.cloned.1.call-start = ((), (), s32[]{:S(2)}) async-start(), calls=%async_computation.1 | async-start | bytes 2359296 | tf_op jit(solution)/shard_map/all_gather | solution.py:120
  18.0 34.3 %copy-start.3 = (s32[2]{0:T(128)}, s32[2]{0:T(128)S(1)}, u32[]{:S(2)}) copy-start(s32[2]{0:T(128)S(1)} %fusion.14.length_ref) | copy-start | bytes 28
  48.7 2.4 %copy-start.1 = (bf16[1024,1024]{1,0:T(8,128)(2,1)S(1)}, bf16[1024,1024]{1,0:T(8,128)(2,1)}, u32[]{:S(2)}) copy-start(bf16[1024,1024]{1,0:T(8,128)(2,1)} %all-gather.2.cloned.1.call-done) | copy-start | bytes 6291460
  53.3 1.4 collective-permute-start
  55.5 5.4 %collective-permute-start.3 = (bf16[2,128,128]{2,1,0:T(8,128)(2,1)S(1)}, bf16[2,128,128]{2,1,0:T(8,128)(2,1)S(1)}, u32[]{:S(2)}, u32[]{:S(2)}) collective-permute-start(bf16[2,128,128]{2,1,0:T(8,128)(2,1)S(1)} %get-tuple-element.26), channel_id=1, source_target_pairs={{0,6},{1,7},{2,0},{3,1},{4,2},{5,3},{6,4},{7,5},{8,14},{9,15},{10,... | collective-permute-start | bytes 196616 | tf_op jit(solution)/shard_map/ppermute | solution.py:105
  57.0 6.4 %collective-permute-start.2 = (bf16[2,128,128]{2,1,0:T(8,128)(2,1)S(1)}, bf16[2,128,128]{2,1,0:T(8,128)(2,1)S(1)}, u32[]{:S(2)}, u32[]{:S(2)}) collective-permute-start(bf16[2,128,128]{2,1,0:T(8,128)(2,1)S(1)} %get-tuple-element.27), channel_id=1, source_target_pairs={{0,4},{1,5},{2,6},{3,7},{4,0},{5,1},{6,2},{7,3},{8,12},{9,13},{10,... | collective-permute-start | bytes 196616 | tf_op jit(solution)/shard_map/ppermute | solution.py:105
  57.9 6.0 %collective-permute-start.1 = (bf16[2,128,128]{2,1,0:T(8,128)(2,1)S(1)}, bf16[2,128,128]{2,1,0:T(8,128)(2,1)S(1)}, u32[]{:S(2)}, u32[]{:S(2)}) collective-permute-start(bf16[2,128,128]{2,1,0:T(8,128)(2,1)S(1)} %get-tuple-element.28), channel_id=1, source_target_pairs={{0,2},{1,3},{2,4},{3,5},{4,6},{5,7},{6,0},{7,1},{8,10},{9,11},{10,... | collective-permute-start | bytes 196616 | tf_op jit(solution)/shard_map/ppermute | solution.py:105
  177.5 1.4 collective-permute-start.4
  179.8 6.2 %collective-permute-start.7 = (bf16[2,128,128]{2,1,0:T(8,128)(2,1)S(1)}, bf16[2,128,128]{2,1,0:T(8,128)(2,1)S(1)}, u32[]{:S(2)}, u32[]{:S(2)}) collective-permute-start(bf16[2,128,128]{2,1,0:T(8,128)(2,1)S(1)} %get-tuple-element.20), channel_id=1, source_target_pairs={{0,6},{1,7},{2,0},{3,1},{4,2},{5,3},{6,4},{7,5},{8,14},{9,15},{10,... | collective-permute-start | bytes 196616 | tf_op jit(solution)/shard_map/ppermute | solution.py:105
  182.8 6.1 %collective-permute-start.6 = (bf16[2,128,128]{2,1,0:T(8,128)(2,1)S(1)}, bf16[2,128,128]{2,1,0:T(8,128)(2,1)S(1)}, u32[]{:S(2)}, u32[]{:S(2)}) collective-permute-start(bf16[2,128,128]{2,1,0:T(8,128)(2,1)S(1)} %get-tuple-element.21), channel_id=1, source_target_pairs={{0,4},{1,5},{2,6},{3,7},{4,0},{5,1},{6,2},{7,3},{8,12},{9,13},{10,... | collective-permute-start | bytes 196616 | tf_op jit(solution)/shard_map/ppermute | solution.py:105
  183.6 6.0 %collective-permute-start.5 = (bf16[2,128,128]{2,1,0:T(8,128)(2,1)S(1)}, bf16[2,128,128]{2,1,0:T(8,128)(2,1)S(1)}, u32[]{:S(2)}, u32[]{:S(2)}) collective-permute-start(bf16[2,128,128]{2,1,0:T(8,128)(2,1)S(1)} %get-tuple-element.22), channel_id=1, source_target_pairs={{0,2},{1,3},{2,4},{3,5},{4,6},{5,7},{6,0},{7,1},{8,10},{9,11},{10,... | collective-permute-start | bytes 196616 | tf_op jit(solution)/shard_map/ppermute | solution.py:105
Sparse Core Ops, SparseCore 0:
  19.7 28.9 all-gather.1

commit v4 on v3

--- a/solution.py
+++ b/solution.py
@@ -110,6 +110,29 @@
     return jnp.transpose(ordered, (2, 0, 1, 3)).reshape(rows, count * width)
 
 
+def gather_rows(values, axis, cores=2):
+    count = lax.axis_size(axis)
+    chips = count // cores
+    me = lax.axis_index(axis)
+    my_chip = me // cores
+    my_core = me % cores
+    swapped = lax.ppermute(values, axis, perm=[(i, i ^ 1) for i in range(count)])
+    both = jnp.stack([values, swapped])
+    pair = jnp.take(both, jnp.stack([my_core, 1 - my_core]), axis=0)
+    received = [pair]
+    for shift in range(1, chips):
+        pairs = [
+            (c * cores + k, ((c + shift) % chips) * cores + k)
+            for c in range(chips)
+            for k in range(cores)
+        ]
+        received.append(lax.ppermute(pair, axis, perm=pairs))
+    stacked = jnp.stack(received)
+    sources = (my_chip - jnp.arange(chips, dtype=jnp.int32)) % chips
+    ordered = jnp.take(stacked, sources, axis=0)
+    return ordered.reshape(count * values.shape[0], values.shape[1])
+
+
 def shards(tokens, w_proj, w_out, kv_cache, slot_request, lengths, block_owner):
     head_local = w_proj.shape[1] // (2 * DH)
     received = lax.all_to_all(kv_cache, "req", split_axis=1, concat_axis=0, tiled=True)
@@ -117,7 +140,7 @@
     pool = received.reshape(-1, BLK, received.shape[-1])
     pool_count = pool.shape[0]
 
-    gathered = lax.all_gather(tokens, "head", axis=0, tiled=True)
+    gathered = gather_rows(tokens, "head")
     normed = layer_norm(gathered.astype(jnp.float32)).astype(jnp.bfloat16)
     row_count = normed.shape[0]
     slots = row_count // CAND

time: 200 us -> 182 us (0.910)
  waiting for transfers between devices: 134 us -> 115 us
  between operations: 13.8 us -> 0.51 us
  starting transfers between devices: 19.1 us -> 27.2 us
  local copies, waits for them, and re-layouts: 9.43 us -> 14.3 us
  other arithmetic: 4.54 us -> 8.49 us
  Pallas kernels: 16 us -> 13.5 us
    all_gather x1 -> x0, waiting for transfers between devices: 28.2 us -> none  [shards(): gathered = lax.all_gather(tokens, 'head', axis=0, tiled=True)]
    ppermute x0 -> x4, waiting for transfers between devices: none -> 20.4 us  [the longest x3 19.9 us: gather_rows(): received.append(lax.ppermute(pair, axis, perm=pairs))]
    all_to_all x1, waiting for transfers between devices: 94.6 us -> 88.9 us  [shards(): lax.all_to_all(kv_cache, 'req', split_axis=1, concat_axis=0, tiled=True)]
    ppermute x0 -> x4, starting transfers between devices: none -> 5.23 us  [the longest x3 5.14 us: gather_rows(): received.append(lax.ppermute(pair, axis, perm=pairs))]
    ppermute x6, waiting for transfers between devices: 8.03 us -> 3.81 us  [exchange(): piece = lax.ppermute(piece, axis, perm=pairs)]
    gather x0 -> x2, local copies, waits for them, and re-layouts: none -> 4.22 us  [the longest x1 3.64 us: gather_rows(): ordered = jnp.take(stacked, sources, axis=0)]
    ppermute x6, starting transfers between devices: 8.23 us -> 11.3 us  [exchange(): piece = lax.ppermute(piece, axis, perm=pairs)]
    another operation x0 -> x2, other arithmetic: none -> 3.02 us  [the longest x1 2.97 us: gather_rows(): stacked = jnp.stack(received)]
  transfers between devices with their start and end apart: 10 -> 13, of which waited for: 9 -> 10; matrix products, arithmetic and copies ran while one was open for 6% -> 11% of each run, Pallas kernels for 0% -> 0%
where the time goes in v4:
time: 182 us
  waiting for transfers between devices  115 us (63%)
  starting transfers between devices  27.2 us (15%)
  local copies, waits for them, and re-layouts  14.3 us (8%)
  Pallas kernels  13.5 us (7%)
  other arithmetic  8.49 us (5%)
  matrix products  2.46 us (1%)
    all_to_all x1, waiting for transfers between devices, shards(): lax.all_to_all(kv_cache, 'req', split_axis=1, concat_axis=0, tiled=True)  88.9 us
    ppermute x3, waiting for transfers between devices, gather_rows(): received.append(lax.ppermute(pair, axis, perm=pairs))  19.9 us
    pallas_call x1, Pallas kernels, attention(): pl.pallas_call(kernel, grid_spec=grid_spec, out_shape=jax.ShapeDtypeStruc...  13.5 us
    ppermute x6, starting transfers between devices, exchange(): piece = lax.ppermute(piece, axis, perm=pairs)  11.3 us
    all_to_all x1, starting transfers between devices, shards(): lax.all_to_all(kv_cache, 'req', split_axis=1, concat_axis=0, tiled=True)  10.4 us
    ppermute x3, starting transfers between devices, gather_rows(): received.append(lax.ppermute(pair, axis, perm=pairs))  5.14 us
    ppermute x6, waiting for transfers between devices, exchange(): piece = lax.ppermute(piece, axis, perm=pairs)  3.81 us
  transfers between devices with their start and end apart: 13, of which 10 were waited for; matrix products, arithmetic and copies ran while one was open for 11% of the time, Pallas kernels for 0%

profile of v4, /device:TPU:112, one launch (start us, length us, event | category | flops | bytes accessed | tf_op | source)
XLA Modules:
  0.0 181.9 jit_solution(14123308128072086118)
XLA Ops:
  0.0 10.4 %all-to-all-start = ((bf16[1,32,3,128,256]{4,3,2,0,1:T(8,128)(2,1)}), bf16[1,32,3,128,256]{4,3,2,0,1:T(8,128)(2,1)}, u32[]{:S(2)}, u32[]{:S(2)}) async-start(bf16[1,32,3,128,256]{4,3,2,0,1:T(8,128)(2,1)} %bitcast.89), calls=%async_computation | async-start | bytes 12582912 | tf_op jit(solution)/shard_map/all_to_all | solution.py:138
  10.9 0.2 fusion.9.length_ref
  11.1 0.2 select_reduce_fusion
  11.6 0.4 collective-permute-done
  12.1 0.6 gather_fusion
  12.9 3.1 %collective-permute-start.2 = (bf16[2,128,1024]{2,1,0:T(8,128)(2,1)S(1)}, bf16[2,128,1024]{2,1,0:T(8,128)(2,1)}, u32[]{:S(2)}, u32[]{:S(2)}) collective-permute-start(bf16[2,128,1024]{2,1,0:T(8,128)(2,1)S(1)} %broadcast_select_fusion.1), channel_id=1, source_target_pairs={{0,4},{1,5},{2,6},{3,7},{4,0},{5,1},{6,2},{7,3},{8,12},{9,13},{10,... | collective-permute-start | bytes 1572872 | tf_op jit(solution)/shard_map/ppermute | solution.py:129
  16.0 1.1 collective-permute-start.3
  17.1 0.9 collective-permute-start.1
  18.4 0.9 gather_fusion.2
  19.3 0.5 and_select_fusion.2.index_ref
  20.0 9.4 %collective-permute-done.2 = bf16[2,128,1024]{2,1,0:T(8,128)(2,1)} collective-permute-done((bf16[2,128,1024]{2,1,0:T(8,128)(2,1)S(1)}, bf16[2,128,1024]{2,1,0:T(8,128)(2,1)}, u32[]{:S(2)}, u32[]{:S(2)}) %collective-permute-start.2) | collective-permute-done | bytes 524320 | tf_op jit(solution)/shard_map/ppermute | solution.py:129
  29.4 10.5 %collective-permute-done.3 = bf16[2,128,1024]{2,1,0:T(8,128)(2,1)} collective-permute-done((bf16[2,128,1024]{2,1,0:T(8,128)(2,1)S(1)}, bf16[2,128,1024]{2,1,0:T(8,128)(2,1)}, u32[]{:S(2)}, u32[]{:S(2)}) %collective-permute-start.3) | collective-permute-done | bytes 524320 | tf_op jit(solution)/shard_map/ppermute | solution.py:129
  39.9 3.0 %pad_maximum_fusion = bf16[4,2,128,1024]{3,2,1,0:T(8,128)(2,1)} fusion(bf16[1,2,128,1024]{3,2,1,0:T(8,128)(2,1)} %bitcast.11, bf16[1,2,128,1024]{3,2,1,0:T(8,128)(2,1)} %bitcast.10, bf16[1,2,128,1024]{3,2,1,0:T(8,128)(2,1)} %bitcast.9, bf16[1,2,128,1024]{3,2,1,0:T(8,128)(2,1)S(1)} %bitcast_select_fusion.1), kind=kLoop, calls=%fused_computation.12 | loop fusion | flops 3145728 | bytes 4194304 | tf_op jit(solution)/shard_map/stack | solution.py:130
  42.9 3.6 %gather_fusion.1 = bf16[4,2,128,1024]{3,2,1,0:T(8,128)(2,1)} fusion(bf16[4,2,128,1024]{3,2,1,0:T(8,128)(2,1)} %pad_maximum_fusion, s32[1024]{0:T(1024)S(1)} %pad_clamp_fusion.2), kind=kCustom, calls=%fused_computation.5 | custom fusion | bytes 4194320 | tf_op jit(solution)/shard_map/jit(_take)/gather | solution.py:132
  46.5 2.6 %convert_reduce_fusion = (f32[4,2,128]{2,1,0:T(2,128)S(1)}, f32[4,2,128]{2,1,0:T(2,128)S(1)}) fusion(bf16[4,2,128,1024]{3,2,1,0:T(8,128)(2,1)} %gather_fusion.1, pred[4]{0:T(512)(128)(4,1)S(1)} %compare_and_fusion), kind=kLoop, calls=%fused_computation.8 | loop fusion | flops 5240832 | bytes 2105348 | tf_op jit(solution)/shard_map/reduce_sum | solution.py:17
  49.1 0.4 bitcast_select_fusion
  49.5 0.6 copy-done.5
  50.2 1.3 multiply_convert_fusion.2
  51.5 0.2 convert_element_type.49
  51.7 0.5 constant_dynamic-slice_fusion.5
  52.8 1.1 collective-permute-done.4
  53.9 0.6 gather_fusion.3
  54.6 1.5 collective-permute-start.5
  56.1 2.7 %collective-permute-start.6 = (bf16[2,128,128]{2,1,0:T(8,128)(2,1)S(1)}, bf16[2,128,128]{2,1,0:T(8,128)(2,1)S(1)}, u32[]{:S(2)}, u32[]{:S(2)}) collective-permute-start(bf16[2,128,128]{2,1,0:T(8,128)(2,1)S(1)} %get-tuple-element.27), channel_id=1, source_target_pairs={{0,4},{1,5},{2,6},{3,7},{4,0},{5,1},{6,2},{7,3},{8,12},{9,13},{10,... | collective-permute-start | bytes 196616 | tf_op jit(solution)/shard_map/ppermute | solution.py:105
  58.8 1.4 collective-permute-start.7
  60.2 0.4 copy.52
  60.6 0.5 concatenate.24
  61.2 0.9 copy.56
  62.1 0.2 collective-permute-done.6
  62.3 0.7 collective-permute-done.7
  63.1 0.6 gather_fusion.4
  63.8 0.2 copy.42
  64.0 88.9 %all-to-all-done = bf16[1,32,3,128,256]{4,3,2,0,1:T(8,128)(2,1)} async-done(((bf16[1,32,3,128,256]{4,3,2,0,1:T(8,128)(2,1)}), bf16[1,32,3,128,256]{4,3,2,0,1:T(8,128)(2,1)}, u32[]{:S(2)}, u32[]{:S(2)}) %all-to-all-start) | async-done | bytes 6291488 | tf_op jit(solution)/shard_map/all_to_all | solution.py:138
  152.9 13.5 %shard_map.73 = bf16[1024,256]{1,0:T(8,128)(2,1)} custom-call(s32[64]{0:T(128)} %and_select_fusion.2.index_ref, s32[2]{0:T(128)} %copy-done.4, bf16[1024,256]{1,0:T(8,128)(2,1)} %bitcast.90, bf16[96,128,256]{2,1,0:T(8,128)(2,1)} %bitcast.31.refs_0_.refs_1_.refs_2_.refs_3_.refs_4_.refs_5_.refs_6_.refs_7_, ...), custom_call_target="tpu_custom_call" | custom-call | tf_op jit(solution)/shard_map/pallas_call | solution.py:74
  166.4 1.2 copy.45
  167.7 0.2 reshape_reshape_squeeze.3
  167.9 0.5 constant_dynamic-slice_fusion.2
  168.9 1.2 collective-permute-done.8
  170.1 0.6 gather_fusion.5
  170.8 1.6 collective-permute-start.9
  172.4 2.7 %collective-permute-start.10 = (bf16[2,128,128]{2,1,0:T(8,128)(2,1)S(1)}, bf16[2,128,128]{2,1,0:T(8,128)(2,1)S(1)}, u32[]{:S(2)}, u32[]{:S(2)}) collective-permute-start(bf16[2,128,128]{2,1,0:T(8,128)(2,1)S(1)} %get-tuple-element.21), channel_id=1, source_target_pairs={{0,4},{1,5},{2,6},{3,7},{4,0},{5,1},{6,2},{7,3},{8,12},{9,13},{10,... | collective-permute-start | bytes 196616 | tf_op jit(solution)/shard_map/ppermute | solution.py:105
  175.1 1.4 collective-permute-start.11
  176.6 2.1 %collective-permute-done.10 = bf16[2,128,128]{2,1,0:T(8,128)(2,1)S(1)} collective-permute-done((bf16[2,128,128]{2,1,0:T(8,128)(2,1)S(1)}, bf16[2,128,128]{2,1,0:T(8,128)(2,1)S(1)}, u32[]{:S(2)}, u32[]{:S(2)}) %collective-permute-start.10) | collective-permute-done | bytes 65568 | tf_op jit(solution)/shard_map/ppermute | solution.py:105
  178.6 0.7 collective-permute-done.11
  179.4 0.6 gather_fusion.6
  180.0 0.2 convert_reduce_fusion.1
  180.4 0.2 copy.49
  180.7 1.2 convolution_convert_fusion
  (68 shorter events, 3.0 us)
Async XLA Ops:
  0.0 180.7 %copy-start = (bf16[1024,1024]{1,0:T(8,128)(2,1)S(1)}, bf16[1024,1024]{1,0:T(8,128)(2,1)}, u32[]{:S(2)}) copy-start(bf16[1024,1024]{1,0:T(8,128)(2,1)} %param.13) | copy-start | bytes 6291460
  0.0 10.5 %copy-start.2 = (bf16[128,1024]{1,0:T(8,128)(2,1)S(1)}, bf16[128,1024]{1,0:T(8,128)(2,1)}, u32[]{:S(2)}) copy-start(bf16[128,1024]{1,0:T(8,128)(2,1)} %param.11) | copy-start | bytes 786436
  0.0 10.6 %copy-start.3 = (s32[64,1]{0,1:T(1,128)S(1)}, s32[64,1]{0,1:T(1,128)}, u32[]{:S(2)}) copy-start(s32[64,1]{0,1:T(1,128)} %param.17) | copy-start | bytes 772
  0.0 10.9 %copy-start.6 = (s32[64]{0:T(128)S(1)}, s32[64]{0:T(128)}, u32[]{:S(2)}) copy-start(s32[64]{0:T(128)} %param.16) | copy-start | bytes 772
  0.0 10.9 %copy-start.7 = (s32[2]{0:T(128)S(1)}, s32[2]{0:T(128)}, u32[]{:S(2)}) copy-start(s32[2]{0:T(128)} %param.15) | copy-start | bytes 28
  0.0 152.9 %all-to-all-start = ((bf16[1,32,3,128,256]{4,3,2,0,1:T(8,128)(2,1)}), bf16[1,32,3,128,256]{4,3,2,0,1:T(8,128)(2,1)}, u32[]{:S(2)}, u32[]{:S(2)}) async-start(bf16[1,32,3,128,256]{4,3,2,0,1:T(8,128)(2,1)} %bitcast.89), calls=%async_computation | async-start | bytes 12582912 | tf_op jit(solution)/shard_map/all_to_all | solution.py:138
  10.5 1.6 collective-permute-start
  11.1 8.2 %copy-start.4 = (s32[2]{0:T(128)}, s32[2]{0:T(128)S(1)}, u32[]{:S(2)}) copy-start(s32[2]{0:T(128)S(1)} %fusion.9.length_ref) | copy-start | bytes 28
  12.9 16.5 %collective-permute-start.2 = (bf16[2,128,1024]{2,1,0:T(8,128)(2,1)S(1)}, bf16[2,128,1024]{2,1,0:T(8,128)(2,1)}, u32[]{:S(2)}, u32[]{:S(2)}) collective-permute-start(bf16[2,128,1024]{2,1,0:T(8,128)(2,1)S(1)} %broadcast_select_fusion.1), channel_id=1, source_target_pairs={{0,4},{1,5},{2,6},{3,7},{4,0},{5,1},{6,2},{7,3},{8,12},{9,13},{10,... | collective-permute-start | bytes 1572872 | tf_op jit(solution)/shard_map/ppermute | solution.py:129
  16.0 23.9 %collective-permute-start.3 = (bf16[2,128,1024]{2,1,0:T(8,128)(2,1)S(1)}, bf16[2,128,1024]{2,1,0:T(8,128)(2,1)}, u32[]{:S(2)}, u32[]{:S(2)}) collective-permute-start(bf16[2,128,1024]{2,1,0:T(8,128)(2,1)S(1)} %broadcast_select_fusion.1), channel_id=1, source_target_pairs={{0,6},{1,7},{2,0},{3,1},{4,2},{5,3},{6,4},{7,5},{8,14},{9,15},{10,... | collective-permute-start | bytes 1572872 | tf_op jit(solution)/shard_map/ppermute | solution.py:129
  17.1 22.8 %collective-permute-start.1 = (bf16[2,128,1024]{2,1,0:T(8,128)(2,1)S(1)}, bf16[2,128,1024]{2,1,0:T(8,128)(2,1)}, u32[]{:S(2)}, u32[]{:S(2)}) collective-permute-start(bf16[2,128,1024]{2,1,0:T(8,128)(2,1)S(1)} %broadcast_select_fusion.1), channel_id=1, source_target_pairs={{0,2},{1,3},{2,4},{3,5},{4,6},{5,7},{6,0},{7,1},{8,10},{9,11},{10,... | collective-permute-start | bytes 1572872 | tf_op jit(solution)/shard_map/ppermute | solution.py:129
  46.5 2.6 %copy-start.1 = (bf16[4,2,128,1024]{3,2,1,0:T(8,128)(2,1)S(1)}, bf16[4,2,128,1024]{3,2,1,0:T(8,128)(2,1)}, u32[]{:S(2)}) copy-start(bf16[4,2,128,1024]{3,2,1,0:T(8,128)(2,1)} %gather_fusion.1) | copy-start | bytes 6291460
  49.1 1.0 copy-start.5
  52.4 1.4 collective-permute-start.4
  54.6 7.4 %collective-permute-start.5 = (bf16[2,128,128]{2,1,0:T(8,128)(2,1)S(1)}, bf16[2,128,128]{2,1,0:T(8,128)(2,1)S(1)}, u32[]{:S(2)}, u32[]{:S(2)}) collective-permute-start(bf16[2,128,128]{2,1,0:T(8,128)(2,1)S(1)} %get-tuple-element.28), channel_id=1, source_target_pairs={{0,2},{1,3},{2,4},{3,5},{4,6},{5,7},{6,0},{7,1},{8,10},{9,11},{10,... | collective-permute-start | bytes 196616 | tf_op jit(solution)/shard_map/ppermute | solution.py:105
  56.1 6.2 %collective-permute-start.6 = (bf16[2,128,128]{2,1,0:T(8,128)(2,1)S(1)}, bf16[2,128,128]{2,1,0:T(8,128)(2,1)S(1)}, u32[]{:S(2)}, u32[]{:S(2)}) collective-permute-start(bf16[2,128,128]{2,1,0:T(8,128)(2,1)S(1)} %get-tuple-element.27), channel_id=1, source_target_pairs={{0,4},{1,5},{2,6},{3,7},{4,0},{5,1},{6,2},{7,3},{8,12},{9,13},{10,... | collective-permute-start | bytes 196616 | tf_op jit(solution)/shard_map/ppermute | solution.py:105
  58.8 4.3 %collective-permute-start.7 = (bf16[2,128,128]{2,1,0:T(8,128)(2,1)S(1)}, bf16[2,128,128]{2,1,0:T(8,128)(2,1)S(1)}, u32[]{:S(2)}, u32[]{:S(2)}) collective-permute-start(bf16[2,128,128]{2,1,0:T(8,128)(2,1)S(1)} %get-tuple-element.26), channel_id=1, source_target_pairs={{0,6},{1,7},{2,0},{3,1},{4,2},{5,3},{6,4},{7,5},{8,14},{9,15},{10,... | collective-permute-start | bytes 196616 | tf_op jit(solution)/shard_map/ppermute | solution.py:105
  168.6 1.4 collective-permute-start.8
  170.8 5.7 %collective-permute-start.9 = (bf16[2,128,128]{2,1,0:T(8,128)(2,1)S(1)}, bf16[2,128,128]{2,1,0:T(8,128)(2,1)S(1)}, u32[]{:S(2)}, u32[]{:S(2)}) collective-permute-start(bf16[2,128,128]{2,1,0:T(8,128)(2,1)S(1)} %get-tuple-element.22), channel_id=1, source_target_pairs={{0,2},{1,3},{2,4},{3,5},{4,6},{5,7},{6,0},{7,1},{8,10},{9,11},{10,... | collective-permute-start | bytes 196616 | tf_op jit(solution)/shard_map/ppermute | solution.py:105
  172.4 6.3 %collective-permute-start.10 = (bf16[2,128,128]{2,1,0:T(8,128)(2,1)S(1)}, bf16[2,128,128]{2,1,0:T(8,128)(2,1)S(1)}, u32[]{:S(2)}, u32[]{:S(2)}) collective-permute-start(bf16[2,128,128]{2,1,0:T(8,128)(2,1)S(1)} %get-tuple-element.21), channel_id=1, source_target_pairs={{0,4},{1,5},{2,6},{3,7},{4,0},{5,1},{6,2},{7,3},{8,12},{9,13},{10,... | collective-permute-start | bytes 196616 | tf_op jit(solution)/shard_map/ppermute | solution.py:105
  175.1 4.3 %collective-permute-start.11 = (bf16[2,128,128]{2,1,0:T(8,128)(2,1)S(1)}, bf16[2,128,128]{2,1,0:T(8,128)(2,1)S(1)}, u32[]{:S(2)}, u32[]{:S(2)}) collective-permute-start(bf16[2,128,128]{2,1,0:T(8,128)(2,1)S(1)} %get-tuple-element.20), channel_id=1, source_target_pairs={{0,6},{1,7},{2,0},{3,1},{4,2},{5,3},{6,4},{7,5},{8,14},{9,15},{10,... | collective-permute-start | bytes 196616 | tf_op jit(solution)/shard_map/ppermute | solution.py:105

commit v5 on v4

--- a/solution.py
+++ b/solution.py
@@ -43,7 +43,7 @@
             query = query_ref[:, lanes]
             half = lax.dot_general(
                 query, pair, (((1,), (1,)), ((), ())), preferred_element_type=jnp.float32
-            ) * (0.5 / DH**0.5)
+            )
             weights = (half + half * jnp.tanh(half)).astype(jnp.bfloat16)
             acc_ref[:, lanes] += jnp.dot(weights, pair, preferred_element_type=jnp.float32)
 
@@ -58,7 +58,7 @@
     )
 
 
-def attention(index, slot_lengths, query_pad, pool, group=8):
+def attention(index, slot_lengths, query_pad, pool, group=16):
     rows, width = query_pad.shape
     slots = rows // CAND
     heads = width // (2 * DH)
@@ -147,7 +147,7 @@
     proj = jax.nn.silu(jnp.dot(normed, w_proj, preferred_element_type=jnp.float32))
     proj = proj.reshape(row_count, head_local, 2, DH)
     gate_u = proj[:, :, 0].astype(jnp.bfloat16).reshape(row_count, head_local * DH)
-    query = proj[:, :, 1].astype(jnp.bfloat16)
+    query = proj[:, :, 1].astype(jnp.bfloat16) * jnp.bfloat16(0.5 / DH**0.5)
     query_pad = jnp.concatenate([query, jnp.zeros_like(query)], axis=2).reshape(
         row_count, head_local * 2 * DH
     )
@@ -171,7 +171,8 @@
     out = attention(index, slot_lengths, query_pad, pool)
     attn = out.reshape(row_count, head_local, 2, DH)[:, :, 1].reshape(row_count, head_local * DH)
 
-    attn_rows = exchange(attn, "head").astype(jnp.float32)
+    attn_rows = lax.all_to_all(attn, "head", split_axis=0, concat_axis=1, tiled=True)
+    attn_rows = attn_rows.astype(jnp.float32)
     gate_rows = gate_rows.astype(jnp.float32)
     hidden = (layer_norm(attn_rows) * gate_rows).astype(jnp.bfloat16)
     return jnp.dot(hidden, w_out, preferred_element_type=jnp.float32).astype(jnp.bfloat16)

time: 182 us -> 179 us (0.984)
  blocking collectives: 0 us -> 11.6 us
  starting transfers between devices: 27.2 us -> 17.4 us
  Pallas kernels: 13.5 us -> 10.6 us
  local copies, waits for them, and re-layouts: 14.3 us -> 11.9 us
    all_to_all x0 -> x1, blocking collectives: none -> 11.6 us  [shards(): lax.all_to_all(attn, 'head', split_axis=0, concat_axis=1, tiled=True)]
    ppermute x6 -> x3, starting transfers between devices: 11.3 us -> 2.3 us  [exchange(): piece = lax.ppermute(piece, axis, perm=pairs)]
    ppermute x3, waiting for transfers between devices: 19.9 us -> 24 us  [gather_rows(): received.append(lax.ppermute(pair, axis, perm=pairs))]
    pallas_call x1, Pallas kernels: 13.5 us -> 10.6 us  [attention(): pl.pallas_call(kernel, grid_spec=grid_spec, out_shape=jax.ShapeDtypeStruc...]
    ppermute x2 -> x1, waiting for transfers between devices: 2.25 us -> 0.28 us  [exchange(): swapped = lax.ppermute(other, axis, perm=[(i, i ^ 1) for i in range(count)])]
    ppermute x6 -> x3, waiting for transfers between devices: 3.81 us -> 2.88 us  [exchange(): piece = lax.ppermute(piece, axis, perm=pairs)]
  transfers between devices with their start and end apart: 13 -> 9, of which waited for: 10 -> 8; matrix products, arithmetic and copies ran while one was open for 11% -> 11% of each run, Pallas kernels for 0% -> 0%
where the time goes in v5:
time: 179 us; the launch traced here: 178 us
  waiting for transfers between devices  115 us (64%)
  starting transfers between devices  17.4 us (10%)
  local copies, waits for them, and re-layouts  11.9 us (7%)
  blocking collectives  11.6 us (6%)
  Pallas kernels  10.6 us (6%)
  other arithmetic  8.15 us (5%)
  matrix products  2.45 us (1%)
    all_to_all x1, waiting for transfers between devices, shards(): lax.all_to_all(kv_cache, 'req', split_axis=1, concat_axis=0, tiled=True)  87.5 us
    ppermute x3, waiting for transfers between devices, gather_rows(): received.append(lax.ppermute(pair, axis, perm=pairs))  24 us
    all_to_all x1, blocking collectives, shards(): lax.all_to_all(attn, 'head', split_axis=0, concat_axis=1, tiled=True)  11.6 us
    pallas_call x1, Pallas kernels, attention(): pl.pallas_call(kernel, grid_spec=grid_spec, out_shape=jax.ShapeDtypeStruc...  10.6 us
    all_to_all x1, starting transfers between devices, shards(): lax.all_to_all(kv_cache, 'req', split_axis=1, concat_axis=0, tiled=True)  10.4 us
    ppermute x3, starting transfers between devices, gather_rows(): received.append(lax.ppermute(pair, axis, perm=pairs))  4.52 us
    gather x1, local copies, waits for them, and re-layouts, gather_rows(): ordered = jnp.take(stacked, sources, axis=0)  3.64 us
  transfers between devices with their start and end apart: 9, of which 8 were waited for; matrix products, arithmetic and copies ran while one was open for 11% of the time, Pallas kernels for 0%

profile of v5, /device:TPU:112, one launch (start us, length us, event | category | flops | bytes accessed | tf_op | source)
XLA Modules:
  0.0 177.9 jit_solution(10387594144827723706)
XLA Ops:
  0.0 10.4 %all-to-all-start = ((bf16[1,32,3,128,256]{4,3,2,0,1:T(8,128)(2,1)}), bf16[1,32,3,128,256]{4,3,2,0,1:T(8,128)(2,1)}, u32[]{:S(2)}, u32[]{:S(2)}) async-start(bf16[1,32,3,128,256]{4,3,2,0,1:T(8,128)(2,1)} %bitcast.76), calls=%async_computation | async-start | bytes 12582912 | tf_op jit(solution)/shard_map/all_to_all | solution.py:138
  10.7 0.1 reduce_window_sum.11
  10.9 0.2 fusion.8.length_ref
  11.1 0.2 select_reduce_fusion
  11.4 0.7 collective-permute-done
  12.1 0.6 gather_fusion
  12.7 0.1 broadcast_select_fusion.1
  12.9 2.8 %collective-permute-start.3 = (bf16[2,128,1024]{2,1,0:T(8,128)(2,1)S(1)}, bf16[2,128,1024]{2,1,0:T(8,128)(2,1)}, u32[]{:S(2)}, u32[]{:S(2)}) collective-permute-start(bf16[2,128,1024]{2,1,0:T(8,128)(2,1)S(1)} %broadcast_select_fusion.1), channel_id=1, source_target_pairs={{0,6},{1,7},{2,0},{3,1},{4,2},{5,3},{6,4},{7,5},{8,14},{9,15},{10,... | collective-permute-start | bytes 1572872 | tf_op jit(solution)/shard_map/ppermute | solution.py:129
  15.7 0.8 collective-permute-start.2
  16.5 0.9 collective-permute-start.1
  18.1 0.1 bitcast_select_fusion.1
  18.2 20.2 %collective-permute-done.3 = bf16[2,128,1024]{2,1,0:T(8,128)(2,1)} collective-permute-done((bf16[2,128,1024]{2,1,0:T(8,128)(2,1)S(1)}, bf16[2,128,1024]{2,1,0:T(8,128)(2,1)}, u32[]{:S(2)}, u32[]{:S(2)}) %collective-permute-start.3) | collective-permute-done | bytes 524320 | tf_op jit(solution)/shard_map/ppermute | solution.py:129
  38.4 3.8 %collective-permute-done.1 = bf16[2,128,1024]{2,1,0:T(8,128)(2,1)} collective-permute-done((bf16[2,128,1024]{2,1,0:T(8,128)(2,1)S(1)}, bf16[2,128,1024]{2,1,0:T(8,128)(2,1)}, u32[]{:S(2)}, u32[]{:S(2)}) %collective-permute-start.1) | collective-permute-done | bytes 524320 | tf_op jit(solution)/shard_map/ppermute | solution.py:129
  42.2 3.0 %pad_maximum_fusion = bf16[4,2,128,1024]{3,2,1,0:T(8,128)(2,1)} fusion(bf16[1,2,128,1024]{3,2,1,0:T(8,128)(2,1)} %bitcast.11, bf16[1,2,128,1024]{3,2,1,0:T(8,128)(2,1)} %bitcast.10, bf16[1,2,128,1024]{3,2,1,0:T(8,128)(2,1)} %bitcast.9, bf16[1,2,128,1024]{3,2,1,0:T(8,128)(2,1)S(1)} %bitcast_select_fusion.1), kind=kLoop, calls=%fused_computation.10 | loop fusion | flops 3145728 | bytes 4194304 | tf_op jit(solution)/shard_map/stack | solution.py:130
  45.2 3.6 %gather_fusion.1 = bf16[4,2,128,1024]{3,2,1,0:T(8,128)(2,1)} fusion(bf16[4,2,128,1024]{3,2,1,0:T(8,128)(2,1)} %pad_maximum_fusion, s32[1024]{0:T(1024)S(1)} %pad_clamp_fusion), kind=kCustom, calls=%fused_computation.1 | custom fusion | bytes 4194320 | tf_op jit(solution)/shard_map/jit(_take)/gather | solution.py:132
  48.8 2.6 %convert_reduce_fusion = (f32[4,2,128]{2,1,0:T(2,128)S(1)}, f32[4,2,128]{2,1,0:T(2,128)S(1)}) fusion(bf16[4,2,128,1024]{3,2,1,0:T(8,128)(2,1)} %gather_fusion.1, pred[4]{0:T(512)(128)(4,1)S(1)} %compare_and_fusion.1), kind=kLoop, calls=%fused_computation.6 | loop fusion | flops 5240832 | bytes 2105348 | tf_op jit(solution)/shard_map/reduce_sum | solution.py:17
  51.5 0.4 bitcast_select_fusion
  51.9 0.6 copy-done.5
  52.5 1.3 multiply_convert_fusion.2
  53.8 0.2 convert_element_type.47
  54.0 0.5 constant_dynamic-slice_fusion.1
  54.6 0.2 copy.33
  54.7 0.1 collective-permute-start.4
  54.8 0.9 gather_fusion.4
  55.7 0.2 copy.41
  55.9 0.3 collective-permute-done.4
  56.2 0.6 gather_fusion.2
  56.8 0.1 broadcast_select_fusion.2
  56.9 0.7 collective-permute-start.7
  57.6 0.8 collective-permute-start.6
  58.4 0.8 collective-permute-start.5
  59.2 0.5 and_select_fusion.2.index_ref
  59.7 0.4 copy.45
  60.1 0.5 concatenate.24
  60.7 0.9 copy.47
  61.6 0.4 collective-permute-done.7
  61.9 1.5 collective-permute-done.6
  63.4 1.0 collective-permute-done.5
  64.5 0.6 gather_fusion.3
  65.1 0.1 select_bitcast_fusion
  65.2 0.2 copy.35
  65.4 87.5 %all-to-all-done = bf16[1,32,3,128,256]{4,3,2,0,1:T(8,128)(2,1)} async-done(((bf16[1,32,3,128,256]{4,3,2,0,1:T(8,128)(2,1)}), bf16[1,32,3,128,256]{4,3,2,0,1:T(8,128)(2,1)}, u32[]{:S(2)}, u32[]{:S(2)}) %all-to-all-start) | async-done | bytes 6291488 | tf_op jit(solution)/shard_map/all_to_all | solution.py:138
  152.9 10.6 %shard_map.73 = bf16[1024,256]{1,0:T(8,128)(2,1)} custom-call(s32[64]{0:T(128)} %and_select_fusion.2.index_ref, s32[2]{0:T(128)} %copy-done.4, bf16[1024,256]{1,0:T(8,128)(2,1)} %bitcast.77, bf16[96,128,256]{2,1,0:T(8,128)(2,1)} %bitcast.31.refs_0_.refs_1_.refs_2_.refs_3_.refs_4_.refs_5_.refs_6_.refs_7_.refs_8_.refs_9_.refs_10_.refs_11_.refs_12_.refs_13_.refs_14_.refs_15_, ...), custom_call_target="tpu_custom_call" | custom-call | tf_op jit(solution)/shard_map/pallas_call | solution.py:74
  163.5 1.2 copy.38
  164.9 11.6 %all_to_all.22 = bf16[8,128,128]{1,2,0:T(8,128)(2,1)S(1)} all-to-all(bf16[8,128,128]{1,2,0:T(8,128)(2,1)S(1)} %copy.39), channel_id=1, replica_groups=mesh['req'=32,'head'=8] {'head'}, dimensions={0} | all-to-all | bytes 524288 | tf_op jit(solution)/shard_map/all_to_all | solution.py:174
  176.5 0.2 convert_reduce_fusion.1
  176.6 0.1 fusion.6
  176.8 1.2 convolution_convert_fusion
  (48 shorter events, 1.4 us)
Async XLA Ops:
  0.0 176.8 %copy-start = (bf16[1024,1024]{1,0:T(8,128)(2,1)S(1)}, bf16[1024,1024]{1,0:T(8,128)(2,1)}, u32[]{:S(2)}) copy-start(bf16[1024,1024]{1,0:T(8,128)(2,1)} %param.9) | copy-start | bytes 6291460
  0.0 10.5 %copy-start.2 = (bf16[128,1024]{1,0:T(8,128)(2,1)S(1)}, bf16[128,1024]{1,0:T(8,128)(2,1)}, u32[]{:S(2)}) copy-start(bf16[128,1024]{1,0:T(8,128)(2,1)} %param.7) | copy-start | bytes 786436
  0.0 10.6 %copy-start.3 = (s32[64,1]{0,1:T(1,128)S(1)}, s32[64,1]{0,1:T(1,128)}, u32[]{:S(2)}) copy-start(s32[64,1]{0,1:T(1,128)} %param.13) | copy-start | bytes 772
  0.0 10.9 %copy-start.6 = (s32[64]{0:T(128)S(1)}, s32[64]{0:T(128)}, u32[]{:S(2)}) copy-start(s32[64]{0:T(128)} %param.12) | copy-start | bytes 772
  0.0 10.9 %copy-start.7 = (s32[2]{0:T(128)S(1)}, s32[2]{0:T(128)}, u32[]{:S(2)}) copy-start(s32[2]{0:T(128)} %param.11) | copy-start | bytes 28
  0.0 152.9 %all-to-all-start = ((bf16[1,32,3,128,256]{4,3,2,0,1:T(8,128)(2,1)}), bf16[1,32,3,128,256]{4,3,2,0,1:T(8,128)(2,1)}, u32[]{:S(2)}, u32[]{:S(2)}) async-start(bf16[1,32,3,128,256]{4,3,2,0,1:T(8,128)(2,1)} %bitcast.76), calls=%async_computation | async-start | bytes 12582912 | tf_op jit(solution)/shard_map/all_to_all | solution.py:138
  10.5 1.6 collective-permute-start
  11.1 7.1 %copy-start.4 = (s32[2]{0:T(128)}, s32[2]{0:T(128)S(1)}, u32[]{:S(2)}) copy-start(s32[2]{0:T(128)S(1)} %fusion.8.length_ref) | copy-start | bytes 28
  12.9 25.6 %collective-permute-start.3 = (bf16[2,128,1024]{2,1,0:T(8,128)(2,1)S(1)}, bf16[2,128,1024]{2,1,0:T(8,128)(2,1)}, u32[]{:S(2)}, u32[]{:S(2)}) collective-permute-start(bf16[2,128,1024]{2,1,0:T(8,128)(2,1)S(1)} %broadcast_select_fusion.1), channel_id=1, source_target_pairs={{0,6},{1,7},{2,0},{3,1},{4,2},{5,3},{6,4},{7,5},{8,14},{9,15},{10,... | collective-permute-start | bytes 1572872 | tf_op jit(solution)/shard_map/ppermute | solution.py:129
  15.7 22.8 %collective-permute-start.2 = (bf16[2,128,1024]{2,1,0:T(8,128)(2,1)S(1)}, bf16[2,128,1024]{2,1,0:T(8,128)(2,1)}, u32[]{:S(2)}, u32[]{:S(2)}) collective-permute-start(bf16[2,128,1024]{2,1,0:T(8,128)(2,1)S(1)} %broadcast_select_fusion.1), channel_id=1, source_target_pairs={{0,4},{1,5},{2,6},{3,7},{4,0},{5,1},{6,2},{7,3},{8,12},{9,13},{10,... | collective-permute-start | bytes 1572872 | tf_op jit(solution)/shard_map/ppermute | solution.py:129
  16.5 25.7 %collective-permute-start.1 = (bf16[2,128,1024]{2,1,0:T(8,128)(2,1)S(1)}, bf16[2,128,1024]{2,1,0:T(8,128)(2,1)}, u32[]{:S(2)}, u32[]{:S(2)}) collective-permute-start(bf16[2,128,1024]{2,1,0:T(8,128)(2,1)S(1)} %broadcast_select_fusion.1), channel_id=1, source_target_pairs={{0,2},{1,3},{2,4},{3,5},{4,6},{5,7},{6,0},{7,1},{8,10},{9,11},{10,... | collective-permute-start | bytes 1572872 | tf_op jit(solution)/shard_map/ppermute | solution.py:129
  48.8 2.6 %copy-start.1 = (bf16[4,2,128,1024]{3,2,1,0:T(8,128)(2,1)S(1)}, bf16[4,2,128,1024]{3,2,1,0:T(8,128)(2,1)}, u32[]{:S(2)}) copy-start(bf16[4,2,128,1024]{3,2,1,0:T(8,128)(2,1)} %gather_fusion.1) | copy-start | bytes 6291460
  51.5 1.0 copy-start.5
  54.7 1.4 collective-permute-start.4
  56.9 5.0 %collective-permute-start.7 = (bf16[2,128,128]{2,1,0:T(8,128)(2,1)S(1)}, bf16[2,128,128]{2,1,0:T(8,128)(2,1)S(1)}, u32[]{:S(2)}, u32[]{:S(2)}) collective-permute-start(bf16[2,128,128]{2,1,0:T(8,128)(2,1)S(1)} %get-tuple-element.18), channel_id=1, source_target_pairs={{0,6},{1,7},{2,0},{3,1},{4,2},{5,3},{6,4},{7,5},{8,14},{9,15},{10,... | collective-permute-start | bytes 196616 | tf_op jit(solution)/shard_map/ppermute | solution.py:105
  57.6 5.8 %collective-permute-start.6 = (bf16[2,128,128]{2,1,0:T(8,128)(2,1)S(1)}, bf16[2,128,128]{2,1,0:T(8,128)(2,1)S(1)}, u32[]{:S(2)}, u32[]{:S(2)}) collective-permute-start(bf16[2,128,128]{2,1,0:T(8,128)(2,1)S(1)} %get-tuple-element.16), channel_id=1, source_target_pairs={{0,4},{1,5},{2,6},{3,7},{4,0},{5,1},{6,2},{7,3},{8,12},{9,13},{10,... | collective-permute-start | bytes 196616 | tf_op jit(solution)/shard_map/ppermute | solution.py:105
  58.4 6.0 %collective-permute-start.5 = (bf16[2,128,128]{2,1,0:T(8,128)(2,1)S(1)}, bf16[2,128,128]{2,1,0:T(8,128)(2,1)S(1)}, u32[]{:S(2)}, u32[]{:S(2)}) collective-permute-start(bf16[2,128,128]{2,1,0:T(8,128)(2,1)S(1)} %get-tuple-element.17), channel_id=1, source_target_pairs={{0,2},{1,3},{2,4},{3,5},{4,6},{5,7},{6,0},{7,1},{8,10},{9,11},{10,... | collective-permute-start | bytes 196616 | tf_op jit(solution)/shard_map/ppermute | solution.py:105

commit v6 on v5

--- a/solution.py
+++ b/solution.py
@@ -5,7 +5,7 @@
 from jax import lax
 from jax.experimental import pallas as pl
 from jax.experimental.pallas import tpu as pltpu
-from jax.sharding import PartitionSpec as P
+from jax.sharding import Mesh, PartitionSpec as P
 
 DH = 64
 CAND = 512
@@ -79,12 +79,30 @@
     )(index, slot_lengths, query_pad, *([pool] * group))
 
 
-def exchange(values, axis, cores=2):
-    count = lax.axis_size(axis)
-    chips = count // cores
-    me = lax.axis_index(axis)
-    my_chip = me // cores
-    my_core = me % cores
+def exchange(values, chip_axis, core_axis):
+    chips = lax.axis_size(chip_axis)
+    cores = lax.axis_size(core_axis)
+    count = chips * cores
+    my_core = lax.axis_index(core_axis)
+    rows = values.shape[0] // count
+    width = values.shape[1]
+    blocks = values.reshape(chips, cores, rows, width)
+    keep = lax.dynamic_index_in_dim(blocks, my_core, 1, keepdims=False)
+    other = lax.dynamic_index_in_dim(blocks, 1 - my_core, 1, keepdims=False)
+    swapped = lax.ppermute(other, (chip_axis, core_axis), perm=[(i, i ^ 1) for i in range(count)])
+    both = jnp.stack([keep, swapped], axis=1)
+    by_source = jnp.take(both, jnp.stack([my_core, 1 - my_core]), axis=1)
+    ordered = lax.all_to_all(by_source, chip_axis, split_axis=0, concat_axis=0, tiled=True)
+    return jnp.transpose(ordered, (2, 0, 1, 3)).reshape(rows, count * width)
+
+
+def exchange_permutes(values, chip_axis, core_axis):
+    chips = lax.axis_size(chip_axis)
+    cores = lax.axis_size(core_axis)
+    count = chips * cores
+    axis = (chip_axis, core_axis)
+    my_chip = lax.axis_index(chip_axis)
+    my_core = lax.axis_index(core_axis)
     rows = values.shape[0] // count
     width = values.shape[1]
     blocks = values.reshape(chips, cores, rows, width)
@@ -110,12 +128,13 @@
     return jnp.transpose(ordered, (2, 0, 1, 3)).reshape(rows, count * width)
 
 
-def gather_rows(values, axis, cores=2):
-    count = lax.axis_size(axis)
-    chips = count // cores
-    me = lax.axis_index(axis)
-    my_chip = me // cores
-    my_core = me % cores
+def gather_rows(values, chip_axis, core_axis):
+    chips = lax.axis_size(chip_axis)
+    cores = lax.axis_size(core_axis)
+    count = chips * cores
+    axis = (chip_axis, core_axis)
+    my_chip = lax.axis_index(chip_axis)
+    my_core = lax.axis_index(core_axis)
     swapped = lax.ppermute(values, axis, perm=[(i, i ^ 1) for i in range(count)])
     both = jnp.stack([values, swapped])
     pair = jnp.take(both, jnp.stack([my_core, 1 - my_core]), axis=0)
@@ -140,7 +159,7 @@
     pool = received.reshape(-1, BLK, received.shape[-1])
     pool_count = pool.shape[0]
 
-    gathered = gather_rows(tokens, "head")
+    gathered = gather_rows(tokens, "hx", "hc")
     normed = layer_norm(gathered.astype(jnp.float32)).astype(jnp.bfloat16)
     row_count = normed.shape[0]
     slots = row_count // CAND
@@ -166,12 +185,12 @@
     blocks = jnp.minimum(jnp.arange(MAXB, dtype=jnp.int32)[None, :], last_live[:, None])
     index = jnp.take_along_axis(index, blocks, axis=1).reshape(-1).astype(jnp.int32)
 
-    gate_rows = exchange(gate_u, "head")
+    gate_rows = exchange_permutes(gate_u, "hx", "hc")
     gate_rows, query_pad = lax.optimization_barrier((gate_rows, query_pad))
     out = attention(index, slot_lengths, query_pad, pool)
     attn = out.reshape(row_count, head_local, 2, DH)[:, :, 1].reshape(row_count, head_local * DH)
 
-    attn_rows = lax.all_to_all(attn, "head", split_axis=0, concat_axis=1, tiled=True)
+    attn_rows = exchange(attn, "hx", "hc")
     attn_rows = attn_rows.astype(jnp.float32)
     gate_rows = gate_rows.astype(jnp.float32)
     hidden = (layer_norm(attn_rows) * gate_rows).astype(jnp.bfloat16)
@@ -179,18 +198,22 @@
 
 
 def solution(mesh):
+    req, head = mesh.devices.shape
+    cores = 2
+    split = Mesh(mesh.devices.reshape(req, head // cores, cores), ("req", "hx", "hc"))
+    heads = ("hx", "hc")
     return jax.shard_map(
         shards,
-        mesh=mesh,
+        mesh=split,
         in_specs=(
-            P(("req", "head"), None),
-            P(None, "head"),
+            P(("req",) + heads, None),
+            P(None, heads),
             P(),
-            P("req", None, None, None, "head"),
+            P("req", None, None, None, heads),
             P("req"),
             P(),
             P("req", None),
         ),
-        out_specs=P(("req", "head"), None),
+        out_specs=P(("req",) + heads, None),
         check_vma=False,
     )

time: 179 us -> 184 us (1.028)
  waiting for transfers between devices: 115 us -> 117 us
    ppermute x4 -> x5, waiting for transfers between devices: 3.17 us -> 4.33 us  [the longest x3 3.14 us: exchange_permutes(): piece = lax.ppermute(piece, axis, perm=pairs)]
  transfers between devices with their start and end apart: 9 -> 10, of which waited for: 8 -> 8; matrix products, arithmetic and copies ran while one was open for 11% -> 11% of each run, Pallas kernels for 0% -> 0%
where the time goes in v6:
time: 184 us; the launch traced here: 181 us
  waiting for transfers between devices  117 us (64%)
  starting transfers between devices  17.5 us (10%)
  local copies, waits for them, and re-layouts  13.7 us (7%)
  Pallas kernels  11.3 us (6%)
  blocking collectives  11.1 us (6%)
  other arithmetic  8.29 us (5%)
  matrix products  2.46 us (1%)
    all_to_all x1, waiting for transfers between devices, shards(): lax.all_to_all(kv_cache, 'req', split_axis=1, concat_axis=0, tiled=True)  87.1 us
    ppermute x3, waiting for transfers between devices, gather_rows(): received.append(lax.ppermute(pair, axis, perm=pairs))  24.4 us
    pallas_call x1, Pallas kernels, attention(): pl.pallas_call(kernel, grid_spec=grid_spec, out_shape=jax.ShapeDtypeStruc...  11.3 us
    all_to_all x1, blocking collectives, exchange(): lax.all_to_all(by_source, chip_axis, split_axis=0, concat_axis=0, tiled=T...  11.1 us
    all_to_all x1, starting transfers between devices, shards(): lax.all_to_all(kv_cache, 'req', split_axis=1, concat_axis=0, tiled=True)  10.4 us
    ppermute x3, starting transfers between devices, gather_rows(): received.append(lax.ppermute(pair, axis, perm=pairs))  4.52 us
  transfers between devices with their start and end apart: 10, of which 8 were waited for; matrix products, arithmetic and copies ran while one was open for 11% of the time, Pallas kernels for 0%

profile of v6, /device:TPU:112, one launch (start us, length us, event | category | flops | bytes accessed | tf_op | source)
XLA Modules:
  0.0 181.3 jit_solution(6421682638013912270)
XLA Ops:
  0.0 10.4 %all-to-all-start = ((bf16[1,32,3,128,256]{4,3,2,0,1:T(8,128)(2,1)}), bf16[1,32,3,128,256]{4,3,2,0,1:T(8,128)(2,1)}, u32[]{:S(2)}, u32[]{:S(2)}) async-start(bf16[1,32,3,128,256]{4,3,2,0,1:T(8,128)(2,1)} %bitcast.80), calls=%async_computation | async-start | bytes 12582912 | tf_op jit(solution)/shard_map/all_to_all | solution.py:157
  10.9 0.2 fusion.8.length_ref
  11.1 0.2 select_reduce_fusion
  11.4 0.7 collective-permute-done
  12.1 0.6 gather_fusion
  12.7 0.1 broadcast_select_fusion.1
  12.9 2.8 %collective-permute-start.3 = (bf16[2,128,1024]{2,1,0:T(8,128)(2,1)S(1)}, bf16[2,128,1024]{2,1,0:T(8,128)(2,1)}, u32[]{:S(2)}, u32[]{:S(2)}) collective-permute-start(bf16[2,128,1024]{2,1,0:T(8,128)(2,1)S(1)} %broadcast_select_fusion.1), channel_id=1, source_target_pairs={{0,6},{1,7},{2,0},{3,1},{4,2},{5,3},{6,4},{7,5},{8,14},{9,15},{10,... | collective-permute-start | bytes 1572872 | tf_op jit(solution)/shard_map/ppermute | solution.py:148
  15.7 0.8 collective-permute-start.2
  16.5 0.9 collective-permute-start.1
  17.8 20.6 %collective-permute-done.3 = bf16[2,128,1024]{2,1,0:T(8,128)(2,1)} collective-permute-done((bf16[2,128,1024]{2,1,0:T(8,128)(2,1)S(1)}, bf16[2,128,1024]{2,1,0:T(8,128)(2,1)}, u32[]{:S(2)}, u32[]{:S(2)}) %collective-permute-start.3) | collective-permute-done | bytes 524320 | tf_op jit(solution)/shard_map/ppermute | solution.py:148
  38.4 3.8 %collective-permute-done.1 = bf16[2,128,1024]{2,1,0:T(8,128)(2,1)} collective-permute-done((bf16[2,128,1024]{2,1,0:T(8,128)(2,1)S(1)}, bf16[2,128,1024]{2,1,0:T(8,128)(2,1)}, u32[]{:S(2)}, u32[]{:S(2)}) %collective-permute-start.1) | collective-permute-done | bytes 524320 | tf_op jit(solution)/shard_map/ppermute | solution.py:148
  42.2 3.0 %pad_maximum_fusion = bf16[4,2,128,1024]{3,2,1,0:T(8,128)(2,1)} fusion(bf16[1,2,128,1024]{3,2,1,0:T(8,128)(2,1)} %bitcast.11, bf16[1,2,128,1024]{3,2,1,0:T(8,128)(2,1)} %bitcast.10, bf16[1,2,128,1024]{3,2,1,0:T(8,128)(2,1)} %bitcast.9, bf16[1,2,128,1024]{3,2,1,0:T(8,128)(2,1)S(1)} %bitcast_select_fusion.1), kind=kLoop, calls=%fused_computation.11 | loop fusion | flops 3145728 | bytes 4194304 | tf_op jit(solution)/shard_map/stack | solution.py:149
  45.2 3.6 %gather_fusion.1 = bf16[4,2,128,1024]{3,2,1,0:T(8,128)(2,1)} fusion(bf16[4,2,128,1024]{3,2,1,0:T(8,128)(2,1)} %pad_maximum_fusion, s32[1024]{0:T(1024)S(1)} %pad_clamp_fusion.1), kind=kCustom, calls=%fused_computation.3 | custom fusion | bytes 4194320 | tf_op jit(solution)/shard_map/jit(_take)/gather | solution.py:151
  48.8 2.6 %convert_reduce_fusion = (f32[4,2,128]{2,1,0:T(2,128)S(1)}, f32[4,2,128]{2,1,0:T(2,128)S(1)}) fusion(bf16[4,2,128,1024]{3,2,1,0:T(8,128)(2,1)} %gather_fusion.1, pred[4]{0:T(512)(128)(4,1)S(1)} %compare_and_fusion.1), kind=kLoop, calls=%fused_computation.7 | loop fusion | flops 5240832 | bytes 2105348 | tf_op jit(solution)/shard_map/reduce_sum | solution.py:17
  51.4 0.4 bitcast_select_fusion
  51.8 0.6 copy-done.5
  52.5 1.3 multiply_convert_fusion.2
  53.8 0.2 convert_element_type.47
  54.0 0.5 constant_dynamic-slice_fusion.4
  54.5 0.2 copy.41
  55.2 0.9 gather_fusion.3
  56.1 0.2 copy.53
  56.3 0.6 gather_fusion.4
  57.0 0.7 collective-permute-start.7
  57.7 0.8 collective-permute-start.6
  58.5 0.8 collective-permute-start.5
  59.3 0.5 and_select_fusion.2.index_ref
  59.9 0.4 copy.57
  60.2 0.5 concatenate.24
  60.8 0.9 copy.59
  61.7 0.3 collective-permute-done.7
  62.0 1.5 collective-permute-done.6
  63.5 1.3 collective-permute-done.5
  64.9 0.6 gather_fusion.2
  65.6 0.2 copy.43
  65.8 87.1 %all-to-all-done = bf16[1,32,3,128,256]{4,3,2,0,1:T(8,128)(2,1)} async-done(((bf16[1,32,3,128,256]{4,3,2,0,1:T(8,128)(2,1)}), bf16[1,32,3,128,256]{4,3,2,0,1:T(8,128)(2,1)}, u32[]{:S(2)}, u32[]{:S(2)}) %all-to-all-start) | async-done | bytes 6291488 | tf_op jit(solution)/shard_map/all_to_all | solution.py:157
  152.9 11.3 %shard_map.73 = bf16[1024,256]{1,0:T(8,128)(2,1)} custom-call(s32[64]{0:T(128)} %and_select_fusion.2.index_ref, s32[2]{0:T(128)} %copy-done.4, bf16[1024,256]{1,0:T(8,128)(2,1)} %bitcast.81, bf16[96,128,256]{2,1,0:T(8,128)(2,1)} %bitcast.31.refs_0_.refs_1_.refs_2_.refs_3_.refs_4_.refs_5_.refs_6_.refs_7_.refs_8_.refs_9_.refs_10_.refs_11_.refs_12_.refs_13_.refs_14_.refs_15_, ...), custom_call_target="tpu_custom_call" | custom-call | tf_op jit(solution)/shard_map/pallas_call | solution.py:74
  164.2 1.2 copy.46
  165.5 0.2 reshape_reshape_squeeze.3
  165.6 0.5 constant_dynamic-slice_fusion.1
  166.2 0.2 copy.48
  166.4 0.2 copy.55
  166.6 1.2 collective-permute-done.8
  167.8 0.6 gather_fusion.5
  168.5 11.1 %all_to_all.14 = bf16[4,2,128,128]{3,2,1,0:T(8,128)(2,1)S(1)} all-to-all(bf16[4,2,128,128]{3,2,1,0:T(8,128)(2,1)S(1)} %copy.50), channel_id=1, replica_groups=mesh['req'=32,'hx'=4,'hc'=2] {'hx'}, dimensions={0} | all-to-all | bytes 524288 | tf_op jit(solution)/shard_map/all_to_all | solution.py:95
  179.6 0.2 copy.51
  179.8 0.2 convert_reduce_fusion.1
  180.1 1.2 convolution_convert_fusion
  (58 shorter events, 2.2 us)
Async XLA Ops:
  0.0 180.1 %copy-start = (bf16[1024,1024]{1,0:T(8,128)(2,1)S(1)}, bf16[1024,1024]{1,0:T(8,128)(2,1)}, u32[]{:S(2)}) copy-start(bf16[1024,1024]{1,0:T(8,128)(2,1)} %param.11) | copy-start | bytes 6291460
  0.0 10.5 %copy-start.2 = (bf16[128,1024]{1,0:T(8,128)(2,1)S(1)}, bf16[128,1024]{1,0:T(8,128)(2,1)}, u32[]{:S(2)}) copy-start(bf16[128,1024]{1,0:T(8,128)(2,1)} %param.9) | copy-start | bytes 786436
  0.0 10.6 %copy-start.3 = (s32[64,1]{0,1:T(1,128)S(1)}, s32[64,1]{0,1:T(1,128)}, u32[]{:S(2)}) copy-start(s32[64,1]{0,1:T(1,128)} %param.15) | copy-start | bytes 772
  0.0 10.9 %copy-start.6 = (s32[64]{0:T(128)S(1)}, s32[64]{0:T(128)}, u32[]{:S(2)}) copy-start(s32[64]{0:T(128)} %param.14) | copy-start | bytes 772
  0.0 10.9 %copy-start.7 = (s32[2]{0:T(128)S(1)}, s32[2]{0:T(128)}, u32[]{:S(2)}) copy-start(s32[2]{0:T(128)} %param.13) | copy-start | bytes 28
  0.0 152.9 %all-to-all-start = ((bf16[1,32,3,128,256]{4,3,2,0,1:T(8,128)(2,1)}), bf16[1,32,3,128,256]{4,3,2,0,1:T(8,128)(2,1)}, u32[]{:S(2)}, u32[]{:S(2)}) async-start(bf16[1,32,3,128,256]{4,3,2,0,1:T(8,128)(2,1)} %bitcast.80), calls=%async_computation | async-start | bytes 12582912 | tf_op jit(solution)/shard_map/all_to_all | solution.py:157
  10.5 1.6 collective-permute-start
  11.1 6.7 %copy-start.4 = (s32[2]{0:T(128)}, s32[2]{0:T(128)S(1)}, u32[]{:S(2)}) copy-start(s32[2]{0:T(128)S(1)} %fusion.8.length_ref) | copy-start | bytes 28
  12.9 25.6 %collective-permute-start.3 = (bf16[2,128,1024]{2,1,0:T(8,128)(2,1)S(1)}, bf16[2,128,1024]{2,1,0:T(8,128)(2,1)}, u32[]{:S(2)}, u32[]{:S(2)}) collective-permute-start(bf16[2,128,1024]{2,1,0:T(8,128)(2,1)S(1)} %broadcast_select_fusion.1), channel_id=1, source_target_pairs={{0,6},{1,7},{2,0},{3,1},{4,2},{5,3},{6,4},{7,5},{8,14},{9,15},{10,... | collective-permute-start | bytes 1572872 | tf_op jit(solution)/shard_map/ppermute | solution.py:148
  15.7 22.8 %collective-permute-start.2 = (bf16[2,128,1024]{2,1,0:T(8,128)(2,1)S(1)}, bf16[2,128,1024]{2,1,0:T(8,128)(2,1)}, u32[]{:S(2)}, u32[]{:S(2)}) collective-permute-start(bf16[2,128,1024]{2,1,0:T(8,128)(2,1)S(1)} %broadcast_select_fusion.1), channel_id=1, source_target_pairs={{0,4},{1,5},{2,6},{3,7},{4,0},{5,1},{6,2},{7,3},{8,12},{9,13},{10,... | collective-permute-start | bytes 1572872 | tf_op jit(solution)/shard_map/ppermute | solution.py:148
  16.5 25.7 %collective-permute-start.1 = (bf16[2,128,1024]{2,1,0:T(8,128)(2,1)S(1)}, bf16[2,128,1024]{2,1,0:T(8,128)(2,1)}, u32[]{:S(2)}, u32[]{:S(2)}) collective-permute-start(bf16[2,128,1024]{2,1,0:T(8,128)(2,1)S(1)} %broadcast_select_fusion.1), channel_id=1, source_target_pairs={{0,2},{1,3},{2,4},{3,5},{4,6},{5,7},{6,0},{7,1},{8,10},{9,11},{10,... | collective-permute-start | bytes 1572872 | tf_op jit(solution)/shard_map/ppermute | solution.py:148
  48.8 2.6 %copy-start.1 = (bf16[4,2,128,1024]{3,2,1,0:T(8,128)(2,1)S(1)}, bf16[4,2,128,1024]{3,2,1,0:T(8,128)(2,1)}, u32[]{:S(2)}) copy-start(bf16[4,2,128,1024]{3,2,1,0:T(8,128)(2,1)} %gather_fusion.1) | copy-start | bytes 6291460
  51.4 1.0 copy-start.5
  54.7 1.6 collective-permute-start.4
  57.0 5.0 %collective-permute-start.7 = (bf16[2,128,128]{2,1,0:T(8,128)(2,1)S(1)}, bf16[2,128,128]{2,1,0:T(8,128)(2,1)S(1)}, u32[]{:S(2)}, u32[]{:S(2)}) collective-permute-start(bf16[2,128,128]{2,1,0:T(8,128)(2,1)S(1)} %get-tuple-element.21), channel_id=1, source_target_pairs={{0,6},{1,7},{2,0},{3,1},{4,2},{5,3},{6,4},{7,5},{8,14},{9,15},{10,... | collective-permute-start | bytes 196616 | tf_op jit(solution)/shard_map/ppermute | solution.py:123
  57.7 5.8 %collective-permute-start.6 = (bf16[2,128,128]{2,1,0:T(8,128)(2,1)S(1)}, bf16[2,128,128]{2,1,0:T(8,128)(2,1)S(1)}, u32[]{:S(2)}, u32[]{:S(2)}) collective-permute-start(bf16[2,128,128]{2,1,0:T(8,128)(2,1)S(1)} %get-tuple-element.22), channel_id=1, source_target_pairs={{0,4},{1,5},{2,6},{3,7},{4,0},{5,1},{6,2},{7,3},{8,12},{9,13},{10,... | collective-permute-start | bytes 196616 | tf_op jit(solution)/shard_map/ppermute | solution.py:123
  58.5 6.3 %collective-permute-start.5 = (bf16[2,128,128]{2,1,0:T(8,128)(2,1)S(1)}, bf16[2,128,128]{2,1,0:T(8,128)(2,1)S(1)}, u32[]{:S(2)}, u32[]{:S(2)}) collective-permute-start(bf16[2,128,128]{2,1,0:T(8,128)(2,1)S(1)} %get-tuple-element.23), channel_id=1, source_target_pairs={{0,2},{1,3},{2,4},{3,5},{4,6},{5,7},{6,0},{7,1},{8,10},{9,11},{10,... | collective-permute-start | bytes 196616 | tf_op jit(solution)/shard_map/ppermute | solution.py:123
  166.3 1.4 collective-permute-start.8

commit v7 on v5

--- a/solution.py
+++ b/solution.py
@@ -49,7 +49,12 @@
 
     @pl.when(step == pl.num_programs(1) - 1)
     def _():
-        out_ref[...] = acc_ref[...].astype(out_ref.dtype)
+        for q in range(CAND // BLK):
+            rows = slice(q * BLK, (q + 1) * BLK)
+            values = jnp.concatenate(
+                [acc_ref[rows, h * 2 * DH + DH : (h + 1) * 2 * DH] for h in range(heads)], axis=1
+            )
+            out_ref[q] = values.T.astype(out_ref.dtype)
 
 
 def pool_spec(width, group, i):
@@ -68,13 +73,15 @@
         grid=(slots, MAXB // group),
         in_specs=[pl.BlockSpec((CAND, width), lambda s, g, idx, lens: (s, 0))]
         + [pool_spec(width, group, i) for i in range(group)],
-        out_specs=pl.BlockSpec((CAND, width), lambda s, g, idx, lens: (s, 0)),
+        out_specs=pl.BlockSpec(
+            (CAND // BLK, heads * DH, BLK), lambda s, g, idx, lens: (s, 0, 0)
+        ),
         scratch_shapes=[pltpu.VMEM((CAND, width), jnp.float32)],
     )
     return pl.pallas_call(
         kernel,
         grid_spec=grid_spec,
-        out_shape=jax.ShapeDtypeStruct((rows, width), jnp.bfloat16),
+        out_shape=jax.ShapeDtypeStruct((rows // BLK, heads * DH, BLK), jnp.bfloat16),
         compiler_params=pltpu.CompilerParams(dimension_semantics=("arbitrary", "arbitrary")),
     )(index, slot_lengths, query_pad, *([pool] * group))
 
@@ -169,7 +176,7 @@
     gate_rows = exchange(gate_u, "head")
     gate_rows, query_pad = lax.optimization_barrier((gate_rows, query_pad))
     out = attention(index, slot_lengths, query_pad, pool)
-    attn = out.reshape(row_count, head_local, 2, DH)[:, :, 1].reshape(row_count, head_local * DH)
+    attn = out.transpose(0, 2, 1).reshape(row_count, head_local * DH)
 
     attn_rows = lax.all_to_all(attn, "head", split_axis=0, concat_axis=1, tiled=True)
     attn_rows = attn_rows.astype(jnp.float32)

time: 179 us -> 178 us (level)
  no operation moved by 1% of the time
where the time goes in v7:
time: 178 us; the launch traced here: 177 us
  waiting for transfers between devices  115 us (65%)
  starting transfers between devices  17.4 us (10%)
  blocking collectives  11.8 us (7%)
  local copies, waits for them, and re-layouts  10.6 us (6%)
  Pallas kernels  10.3 us (6%)
  other arithmetic  8.21 us (5%)
  matrix products  2.45 us (1%)
    all_to_all x1, waiting for transfers between devices, shards(): lax.all_to_all(kv_cache, 'req', split_axis=1, concat_axis=0, tiled=True)  87.5 us
    ppermute x3, waiting for transfers between devices, gather_rows(): received.append(lax.ppermute(pair, axis, perm=pairs))  24 us
    all_to_all x1, blocking collectives, shards(): lax.all_to_all(attn, 'head', split_axis=0, concat_axis=1, tiled=True)  11.8 us
    all_to_all x1, starting transfers between devices, shards(): lax.all_to_all(kv_cache, 'req', split_axis=1, concat_axis=0, tiled=True)  10.4 us
    pallas_call x1, Pallas kernels, attention(): pl.pallas_call(kernel, grid_spec=grid_spec, out_shape=jax.ShapeDtypeStruc...  10.3 us
    ppermute x3, starting transfers between devices, gather_rows(): received.append(lax.ppermute(pair, axis, perm=pairs))  4.52 us
    gather x1, local copies, waits for them, and re-layouts, gather_rows(): ordered = jnp.take(stacked, sources, axis=0)  3.64 us
  transfers between devices with their start and end apart: 9, of which 8 were waited for; matrix products, arithmetic and copies ran while one was open for 11% of the time, Pallas kernels for 0%

profile of v7, /device:TPU:112, one launch (start us, length us, event | category | flops | bytes accessed | tf_op | source)
XLA Modules:
  0.0 176.6 jit_solution(9241101271875295377)
XLA Ops:
  0.0 10.4 %all-to-all-start = ((bf16[1,32,3,128,256]{4,3,2,0,1:T(8,128)(2,1)}), bf16[1,32,3,128,256]{4,3,2,0,1:T(8,128)(2,1)}, u32[]{:S(2)}, u32[]{:S(2)}) async-start(bf16[1,32,3,128,256]{4,3,2,0,1:T(8,128)(2,1)} %bitcast.70), calls=%async_computation | async-start | bytes 12582912 | tf_op jit(solution)/shard_map/all_to_all | solution.py:145
  10.5 0.1 collective-permute-start
  10.7 0.1 reduce_window_sum.11
  10.9 0.2 fusion.8.length_ref
  11.1 0.2 select_reduce_fusion
  11.4 0.7 collective-permute-done
  12.1 0.6 gather_fusion
  12.7 0.1 broadcast_select_fusion.1
  12.9 2.8 %collective-permute-start.3 = (bf16[2,128,1024]{2,1,0:T(8,128)(2,1)S(1)}, bf16[2,128,1024]{2,1,0:T(8,128)(2,1)}, u32[]{:S(2)}, u32[]{:S(2)}) collective-permute-start(bf16[2,128,1024]{2,1,0:T(8,128)(2,1)S(1)} %broadcast_select_fusion.1), channel_id=1, source_target_pairs={{0,6},{1,7},{2,0},{3,1},{4,2},{5,3},{6,4},{7,5},{8,14},{9,15},{10,... | collective-permute-start | bytes 1572872 | tf_op jit(solution)/shard_map/ppermute | solution.py:136
  15.7 0.8 collective-permute-start.2
  16.5 0.9 collective-permute-start.1
  18.1 0.1 bitcast_select_fusion.1
  18.2 20.2 %collective-permute-done.3 = bf16[2,128,1024]{2,1,0:T(8,128)(2,1)} collective-permute-done((bf16[2,128,1024]{2,1,0:T(8,128)(2,1)S(1)}, bf16[2,128,1024]{2,1,0:T(8,128)(2,1)}, u32[]{:S(2)}, u32[]{:S(2)}) %collective-permute-start.3) | collective-permute-done | bytes 524320 | tf_op jit(solution)/shard_map/ppermute | solution.py:136
  38.4 3.8 %collective-permute-done.1 = bf16[2,128,1024]{2,1,0:T(8,128)(2,1)} collective-permute-done((bf16[2,128,1024]{2,1,0:T(8,128)(2,1)S(1)}, bf16[2,128,1024]{2,1,0:T(8,128)(2,1)}, u32[]{:S(2)}, u32[]{:S(2)}) %collective-permute-start.1) | collective-permute-done | bytes 524320 | tf_op jit(solution)/shard_map/ppermute | solution.py:136
  42.2 3.0 %pad_maximum_fusion = bf16[4,2,128,1024]{3,2,1,0:T(8,128)(2,1)} fusion(bf16[1,2,128,1024]{3,2,1,0:T(8,128)(2,1)} %bitcast.11, bf16[1,2,128,1024]{3,2,1,0:T(8,128)(2,1)} %bitcast.10, bf16[1,2,128,1024]{3,2,1,0:T(8,128)(2,1)} %bitcast.9, bf16[1,2,128,1024]{3,2,1,0:T(8,128)(2,1)S(1)} %bitcast_select_fusion.1), kind=kLoop, calls=%fused_computation.10 | loop fusion | flops 3145728 | bytes 4194304 | tf_op jit(solution)/shard_map/stack | solution.py:137
  45.2 3.6 %gather_fusion.1 = bf16[4,2,128,1024]{3,2,1,0:T(8,128)(2,1)} fusion(bf16[4,2,128,1024]{3,2,1,0:T(8,128)(2,1)} %pad_maximum_fusion, s32[1024]{0:T(1024)S(1)} %pad_clamp_fusion), kind=kCustom, calls=%fused_computation.1 | custom fusion | bytes 4194320 | tf_op jit(solution)/shard_map/jit(_take)/gather | solution.py:139
  48.8 2.6 %convert_reduce_fusion = (f32[4,2,128]{2,1,0:T(2,128)S(1)}, f32[4,2,128]{2,1,0:T(2,128)S(1)}) fusion(bf16[4,2,128,1024]{3,2,1,0:T(8,128)(2,1)} %gather_fusion.1, pred[4]{0:T(512)(128)(4,1)S(1)} %compare_and_fusion.1), kind=kLoop, calls=%fused_computation.6 | loop fusion | flops 5240832 | bytes 2105348 | tf_op jit(solution)/shard_map/reduce_sum | solution.py:17
  51.5 0.4 bitcast_select_fusion
  51.9 0.6 copy-done.5
  52.5 1.3 multiply_convert_fusion.2
  53.8 0.2 convert_element_type.47
  54.0 0.5 constant_dynamic-slice_fusion.1
  54.6 0.2 copy.27
  54.7 0.1 collective-permute-start.4
  54.8 0.9 gather_fusion.4
  55.7 0.2 copy.33
  55.9 0.3 collective-permute-done.4
  56.2 0.6 gather_fusion.2
  56.8 0.1 broadcast_select_fusion.2
  56.9 0.7 collective-permute-start.7
  57.6 0.8 collective-permute-start.6
  58.4 0.8 collective-permute-start.5
  59.2 0.6 and_select_fusion.2.index_ref
  59.8 0.4 copy.36
  60.2 0.5 concatenate.24
  60.7 0.9 copy.38
  61.6 0.3 collective-permute-done.7
  61.9 1.5 collective-permute-done.6
  63.4 1.0 collective-permute-done.5
  64.5 0.6 gather_fusion.3
  65.1 0.1 select_bitcast_fusion
  65.2 0.2 copy.29
  65.4 87.5 %all-to-all-done = bf16[1,32,3,128,256]{4,3,2,0,1:T(8,128)(2,1)} async-done(((bf16[1,32,3,128,256]{4,3,2,0,1:T(8,128)(2,1)}), bf16[1,32,3,128,256]{4,3,2,0,1:T(8,128)(2,1)}, u32[]{:S(2)}, u32[]{:S(2)}) %all-to-all-start) | async-done | bytes 6291488 | tf_op jit(solution)/shard_map/all_to_all | solution.py:145
  152.9 10.3 %shard_map.73 = bf16[8,128,128]{2,1,0:T(8,128)(2,1)} custom-call(s32[64]{0:T(128)} %and_select_fusion.2.index_ref, s32[2]{0:T(128)} %copy-done.4, bf16[1024,256]{1,0:T(8,128)(2,1)} %bitcast.71, ...), custom_call_target="tpu_custom_call" | custom-call | tf_op jit(solution)/shard_map/pallas_call | solution.py:81
  163.3 11.8 %all_to_all.9 = bf16[8,128,128]{1,2,0:T(8,128)(2,1)S(1)} all-to-all(bf16[8,128,128]{1,2,0:T(8,128)(2,1)} %bitcast.74), channel_id=1, replica_groups=mesh['req'=32,'head'=8] {'head'}, dimensions={0} | all-to-all | bytes 524288 | tf_op jit(solution)/shard_map/all_to_all | solution.py:181
  175.1 0.2 convert_reduce_fusion.1
  175.3 0.1 fusion.6
  175.4 1.2 convolution_convert_fusion
  (44 shorter events, 1.2 us)
Async XLA Ops:
  0.0 175.4 %copy-start = (bf16[1024,1024]{1,0:T(8,128)(2,1)S(1)}, bf16[1024,1024]{1,0:T(8,128)(2,1)}, u32[]{:S(2)}) copy-start(bf16[1024,1024]{1,0:T(8,128)(2,1)} %param.9) | copy-start | bytes 6291460
  0.0 10.5 %copy-start.2 = (bf16[128,1024]{1,0:T(8,128)(2,1)S(1)}, bf16[128,1024]{1,0:T(8,128)(2,1)}, u32[]{:S(2)}) copy-start(bf16[128,1024]{1,0:T(8,128)(2,1)} %param.7) | copy-start | bytes 786436
  0.0 10.6 %copy-start.3 = (s32[64,1]{0,1:T(1,128)S(1)}, s32[64,1]{0,1:T(1,128)}, u32[]{:S(2)}) copy-start(s32[64,1]{0,1:T(1,128)} %param.13) | copy-start | bytes 772
  0.0 10.9 %copy-start.6 = (s32[64]{0:T(128)S(1)}, s32[64]{0:T(128)}, u32[]{:S(2)}) copy-start(s32[64]{0:T(128)} %param.12) | copy-start | bytes 772
  0.0 10.9 %copy-start.7 = (s32[2]{0:T(128)S(1)}, s32[2]{0:T(128)}, u32[]{:S(2)}) copy-start(s32[2]{0:T(128)} %param.11) | copy-start | bytes 28
  0.0 152.9 %all-to-all-start = ((bf16[1,32,3,128,256]{4,3,2,0,1:T(8,128)(2,1)}), bf16[1,32,3,128,256]{4,3,2,0,1:T(8,128)(2,1)}, u32[]{:S(2)}, u32[]{:S(2)}) async-start(bf16[1,32,3,128,256]{4,3,2,0,1:T(8,128)(2,1)} %bitcast.70), calls=%async_computation | async-start | bytes 12582912 | tf_op jit(solution)/shard_map/all_to_all | solution.py:145
  10.5 1.6 collective-permute-start
  11.1 7.1 %copy-start.4 = (s32[2]{0:T(128)}, s32[2]{0:T(128)S(1)}, u32[]{:S(2)}) copy-start(s32[2]{0:T(128)S(1)} %fusion.8.length_ref) | copy-start | bytes 28
  12.9 25.6 %collective-permute-start.3 = (bf16[2,128,1024]{2,1,0:T(8,128)(2,1)S(1)}, bf16[2,128,1024]{2,1,0:T(8,128)(2,1)}, u32[]{:S(2)}, u32[]{:S(2)}) collective-permute-start(bf16[2,128,1024]{2,1,0:T(8,128)(2,1)S(1)} %broadcast_select_fusion.1), channel_id=1, source_target_pairs={{0,6},{1,7},{2,0},{3,1},{4,2},{5,3},{6,4},{7,5},{8,14},{9,15},{10,... | collective-permute-start | bytes 1572872 | tf_op jit(solution)/shard_map/ppermute | solution.py:136
  15.7 22.8 %collective-permute-start.2 = (bf16[2,128,1024]{2,1,0:T(8,128)(2,1)S(1)}, bf16[2,128,1024]{2,1,0:T(8,128)(2,1)}, u32[]{:S(2)}, u32[]{:S(2)}) collective-permute-start(bf16[2,128,1024]{2,1,0:T(8,128)(2,1)S(1)} %broadcast_select_fusion.1), channel_id=1, source_target_pairs={{0,4},{1,5},{2,6},{3,7},{4,0},{5,1},{6,2},{7,3},{8,12},{9,13},{10,... | collective-permute-start | bytes 1572872 | tf_op jit(solution)/shard_map/ppermute | solution.py:136
  16.5 25.7 %collective-permute-start.1 = (bf16[2,128,1024]{2,1,0:T(8,128)(2,1)S(1)}, bf16[2,128,1024]{2,1,0:T(8,128)(2,1)}, u32[]{:S(2)}, u32[]{:S(2)}) collective-permute-start(bf16[2,128,1024]{2,1,0:T(8,128)(2,1)S(1)} %broadcast_select_fusion.1), channel_id=1, source_target_pairs={{0,2},{1,3},{2,4},{3,5},{4,6},{5,7},{6,0},{7,1},{8,10},{9,11},{10,... | collective-permute-start | bytes 1572872 | tf_op jit(solution)/shard_map/ppermute | solution.py:136
  48.8 2.6 %copy-start.1 = (bf16[4,2,128,1024]{3,2,1,0:T(8,128)(2,1)S(1)}, bf16[4,2,128,1024]{3,2,1,0:T(8,128)(2,1)}, u32[]{:S(2)}) copy-start(bf16[4,2,128,1024]{3,2,1,0:T(8,128)(2,1)} %gather_fusion.1) | copy-start | bytes 6291460
  51.5 1.0 copy-start.5
  54.7 1.4 collective-permute-start.4
  56.9 5.0 %collective-permute-start.7 = (bf16[2,128,128]{2,1,0:T(8,128)(2,1)S(1)}, bf16[2,128,128]{2,1,0:T(8,128)(2,1)S(1)}, u32[]{:S(2)}, u32[]{:S(2)}) collective-permute-start(bf16[2,128,128]{2,1,0:T(8,128)(2,1)S(1)} %get-tuple-element.18), channel_id=1, source_target_pairs={{0,6},{1,7},{2,0},{3,1},{4,2},{5,3},{6,4},{7,5},{8,14},{9,15},{10,... | collective-permute-start | bytes 196616 | tf_op jit(solution)/shard_map/ppermute | solution.py:112
  57.6 5.8 %collective-permute-start.6 = (bf16[2,128,128]{2,1,0:T(8,128)(2,1)S(1)}, bf16[2,128,128]{2,1,0:T(8,128)(2,1)S(1)}, u32[]{:S(2)}, u32[]{:S(2)}) collective-permute-start(bf16[2,128,128]{2,1,0:T(8,128)(2,1)S(1)} %get-tuple-element.16), channel_id=1, source_target_pairs={{0,4},{1,5},{2,6},{3,7},{4,0},{5,1},{6,2},{7,3},{8,12},{9,13},{10,... | collective-permute-start | bytes 196616 | tf_op jit(solution)/shard_map/ppermute | solution.py:112
  58.4 6.0 %collective-permute-start.5 = (bf16[2,128,128]{2,1,0:T(8,128)(2,1)S(1)}, bf16[2,128,128]{2,1,0:T(8,128)(2,1)S(1)}, u32[]{:S(2)}, u32[]{:S(2)}) collective-permute-start(bf16[2,128,128]{2,1,0:T(8,128)(2,1)S(1)} %get-tuple-element.17), channel_id=1, source_target_pairs={{0,2},{1,3},{2,4},{3,5},{4,6},{5,7},{6,0},{7,1},{8,10},{9,11},{10,... | collective-permute-start | bytes 196616 | tf_op jit(solution)/shard_map/ppermute | solution.py:112

commit v8 on v7

--- a/solution.py
+++ b/solution.py
@@ -63,7 +63,7 @@
     )
 
 
-def attention(index, slot_lengths, query_pad, pool, group=16):
+def attention(index, slot_lengths, query_pad, pool, group=32):
     rows, width = query_pad.shape
     slots = rows // CAND
     heads = width // (2 * DH)

time: 178 us -> 182 us (1.022)
  Pallas kernels: 10.3 us -> 13.7 us
    pallas_call x1, Pallas kernels: 10.3 us -> 13.7 us  [attention(): pl.pallas_call(kernel, grid_spec=grid_spec, out_shape=jax.ShapeDtypeStruc...]
where the time goes in v8:
time: 182 us; the launch traced here: 180 us
  waiting for transfers between devices  115 us (63%)
  starting transfers between devices  17.4 us (10%)
  Pallas kernels  13.7 us (8%)
  blocking collectives  11.8 us (6%)
  local copies, waits for them, and re-layouts  10.6 us (6%)
  other arithmetic  8.21 us (5%)
  matrix products  2.45 us (1%)
    all_to_all x1, waiting for transfers between devices, shards(): lax.all_to_all(kv_cache, 'req', split_axis=1, concat_axis=0, tiled=True)  87.5 us
    ppermute x3, waiting for transfers between devices, gather_rows(): received.append(lax.ppermute(pair, axis, perm=pairs))  24 us
    pallas_call x1, Pallas kernels, attention(): pl.pallas_call(kernel, grid_spec=grid_spec, out_shape=jax.ShapeDtypeStruc...  13.7 us
    all_to_all x1, blocking collectives, shards(): lax.all_to_all(attn, 'head', split_axis=0, concat_axis=1, tiled=True)  11.8 us
    all_to_all x1, starting transfers between devices, shards(): lax.all_to_all(kv_cache, 'req', split_axis=1, concat_axis=0, tiled=True)  10.4 us
    ppermute x3, starting transfers between devices, gather_rows(): received.append(lax.ppermute(pair, axis, perm=pairs))  4.52 us
    gather x1, local copies, waits for them, and re-layouts, gather_rows(): ordered = jnp.take(stacked, sources, axis=0)  3.64 us
  transfers between devices with their start and end apart: 9, of which 8 were waited for; matrix products, arithmetic and copies ran while one was open for 11% of the time, Pallas kernels for 0%

profile of v8, /device:TPU:112, one launch (start us, length us, event | category | flops | bytes accessed | tf_op | source)
XLA Modules:
  0.0 179.9 jit_solution(7872753173014035705)
XLA Ops:
  0.0 10.4 %all-to-all-start = ((bf16[1,32,3,128,256]{4,3,2,0,1:T(8,128)(2,1)}), bf16[1,32,3,128,256]{4,3,2,0,1:T(8,128)(2,1)}, u32[]{:S(2)}, u32[]{:S(2)}) async-start(bf16[1,32,3,128,256]{4,3,2,0,1:T(8,128)(2,1)} %bitcast.70), calls=%async_computation | async-start | bytes 12582912 | tf_op jit(solution)/shard_map/all_to_all | solution.py:145
  10.5 0.1 collective-permute-start
  10.7 0.1 reduce_window_sum.11
  10.9 0.2 fusion.8.length_ref
  11.1 0.2 select_reduce_fusion
  11.4 0.7 collective-permute-done
  12.1 0.6 gather_fusion
  12.7 0.1 broadcast_select_fusion.1
  12.9 2.8 %collective-permute-start.3 = (bf16[2,128,1024]{2,1,0:T(8,128)(2,1)S(1)}, bf16[2,128,1024]{2,1,0:T(8,128)(2,1)}, u32[]{:S(2)}, u32[]{:S(2)}) collective-permute-start(bf16[2,128,1024]{2,1,0:T(8,128)(2,1)S(1)} %broadcast_select_fusion.1), channel_id=1, source_target_pairs={{0,6},{1,7},{2,0},{3,1},{4,2},{5,3},{6,4},{7,5},{8,14},{9,15},{10,... | collective-permute-start | bytes 1572872 | tf_op jit(solution)/shard_map/ppermute | solution.py:136
  15.7 0.8 collective-permute-start.2
  16.5 0.9 collective-permute-start.1
  18.1 0.1 bitcast_select_fusion.1
  18.2 20.2 %collective-permute-done.3 = bf16[2,128,1024]{2,1,0:T(8,128)(2,1)} collective-permute-done((bf16[2,128,1024]{2,1,0:T(8,128)(2,1)S(1)}, bf16[2,128,1024]{2,1,0:T(8,128)(2,1)}, u32[]{:S(2)}, u32[]{:S(2)}) %collective-permute-start.3) | collective-permute-done | bytes 524320 | tf_op jit(solution)/shard_map/ppermute | solution.py:136
  38.4 3.8 %collective-permute-done.1 = bf16[2,128,1024]{2,1,0:T(8,128)(2,1)} collective-permute-done((bf16[2,128,1024]{2,1,0:T(8,128)(2,1)S(1)}, bf16[2,128,1024]{2,1,0:T(8,128)(2,1)}, u32[]{:S(2)}, u32[]{:S(2)}) %collective-permute-start.1) | collective-permute-done | bytes 524320 | tf_op jit(solution)/shard_map/ppermute | solution.py:136
  42.2 3.0 %pad_maximum_fusion = bf16[4,2,128,1024]{3,2,1,0:T(8,128)(2,1)} fusion(bf16[1,2,128,1024]{3,2,1,0:T(8,128)(2,1)} %bitcast.11, bf16[1,2,128,1024]{3,2,1,0:T(8,128)(2,1)} %bitcast.10, bf16[1,2,128,1024]{3,2,1,0:T(8,128)(2,1)} %bitcast.9, bf16[1,2,128,1024]{3,2,1,0:T(8,128)(2,1)S(1)} %bitcast_select_fusion.1), kind=kLoop, calls=%fused_computation.10 | loop fusion | flops 3145728 | bytes 4194304 | tf_op jit(solution)/shard_map/stack | solution.py:137
  45.2 3.6 %gather_fusion.1 = bf16[4,2,128,1024]{3,2,1,0:T(8,128)(2,1)} fusion(bf16[4,2,128,1024]{3,2,1,0:T(8,128)(2,1)} %pad_maximum_fusion, s32[1024]{0:T(1024)S(1)} %pad_clamp_fusion), kind=kCustom, calls=%fused_computation.1 | custom fusion | bytes 4194320 | tf_op jit(solution)/shard_map/jit(_take)/gather | solution.py:139
  48.8 2.6 %convert_reduce_fusion = (f32[4,2,128]{2,1,0:T(2,128)S(1)}, f32[4,2,128]{2,1,0:T(2,128)S(1)}) fusion(bf16[4,2,128,1024]{3,2,1,0:T(8,128)(2,1)} %gather_fusion.1, pred[4]{0:T(512)(128)(4,1)S(1)} %compare_and_fusion.1), kind=kLoop, calls=%fused_computation.6 | loop fusion | flops 5240832 | bytes 2105348 | tf_op jit(solution)/shard_map/reduce_sum | solution.py:17
  51.5 0.4 bitcast_select_fusion
  51.9 0.6 copy-done.5
  52.5 1.3 multiply_convert_fusion.2
  53.8 0.2 convert_element_type.47
  54.0 0.5 constant_dynamic-slice_fusion.1
  54.6 0.2 copy.27
  54.7 0.1 collective-permute-start.4
  54.8 0.9 gather_fusion.4
  55.7 0.2 copy.33
  55.9 0.3 collective-permute-done.4
  56.2 0.6 gather_fusion.2
  56.8 0.1 broadcast_select_fusion.2
  56.9 0.7 collective-permute-start.7
  57.6 0.8 collective-permute-start.6
  58.4 0.8 collective-permute-start.5
  59.2 0.6 and_select_fusion.2.index_ref
  59.8 0.4 copy.36
  60.2 0.5 concatenate.24
  60.7 0.9 copy.38
  61.6 0.3 collective-permute-done.7
  61.9 1.5 collective-permute-done.6
  63.4 1.0 collective-permute-done.5
  64.5 0.6 gather_fusion.3
  65.1 0.1 select_bitcast_fusion
  65.2 0.2 copy.29
  65.4 87.5 %all-to-all-done = bf16[1,32,3,128,256]{4,3,2,0,1:T(8,128)(2,1)} async-done(((bf16[1,32,3,128,256]{4,3,2,0,1:T(8,128)(2,1)}), bf16[1,32,3,128,256]{4,3,2,0,1:T(8,128)(2,1)}, u32[]{:S(2)}, u32[]{:S(2)}) %all-to-all-start) | async-done | bytes 6291488 | tf_op jit(solution)/shard_map/all_to_all | solution.py:145
  152.9 13.7 %shard_map.73 = bf16[8,128,128]{2,1,0:T(8,128)(2,1)} custom-call(s32[64]{0:T(128)} %and_select_fusion.2.index_ref, s32[2]{0:T(128)} %copy-done.4, bf16[1024,256]{1,0:T(8,128)(2,1)} %bitcast.71, ...), custom_call_target="tpu_custom_call" | custom-call | tf_op jit(solution)/shard_map/pallas_call | solution.py:81
  166.6 11.8 %all_to_all.9 = bf16[8,128,128]{1,2,0:T(8,128)(2,1)S(1)} all-to-all(bf16[8,128,128]{1,2,0:T(8,128)(2,1)} %bitcast.74), channel_id=1, replica_groups=mesh['req'=32,'head'=8] {'head'}, dimensions={0} | all-to-all | bytes 524288 | tf_op jit(solution)/shard_map/all_to_all | solution.py:181
  178.5 0.2 convert_reduce_fusion.1
  178.6 0.1 fusion.6
  178.7 1.2 convolution_convert_fusion
  (44 shorter events, 1.2 us)
Async XLA Ops:
  0.0 178.7 %copy-start = (bf16[1024,1024]{1,0:T(8,128)(2,1)S(1)}, bf16[1024,1024]{1,0:T(8,128)(2,1)}, u32[]{:S(2)}) copy-start(bf16[1024,1024]{1,0:T(8,128)(2,1)} %param.9) | copy-start | bytes 6291460
  0.0 10.5 %copy-start.2 = (bf16[128,1024]{1,0:T(8,128)(2,1)S(1)}, bf16[128,1024]{1,0:T(8,128)(2,1)}, u32[]{:S(2)}) copy-start(bf16[128,1024]{1,0:T(8,128)(2,1)} %param.7) | copy-start | bytes 786436
  0.0 10.6 %copy-start.3 = (s32[64,1]{0,1:T(1,128)S(1)}, s32[64,1]{0,1:T(1,128)}, u32[]{:S(2)}) copy-start(s32[64,1]{0,1:T(1,128)} %param.13) | copy-start | bytes 772
  0.0 10.9 %copy-start.6 = (s32[64]{0:T(128)S(1)}, s32[64]{0:T(128)}, u32[]{:S(2)}) copy-start(s32[64]{0:T(128)} %param.12) | copy-start | bytes 772
  0.0 10.9 %copy-start.7 = (s32[2]{0:T(128)S(1)}, s32[2]{0:T(128)}, u32[]{:S(2)}) copy-start(s32[2]{0:T(128)} %param.11) | copy-start | bytes 28
  0.0 152.9 %all-to-all-start = ((bf16[1,32,3,128,256]{4,3,2,0,1:T(8,128)(2,1)}), bf16[1,32,3,128,256]{4,3,2,0,1:T(8,128)(2,1)}, u32[]{:S(2)}, u32[]{:S(2)}) async-start(bf16[1,32,3,128,256]{4,3,2,0,1:T(8,128)(2,1)} %bitcast.70), calls=%async_computation | async-start | bytes 12582912 | tf_op jit(solution)/shard_map/all_to_all | solution.py:145
  10.5 1.6 collective-permute-start
  11.1 7.1 %copy-start.4 = (s32[2]{0:T(128)}, s32[2]{0:T(128)S(1)}, u32[]{:S(2)}) copy-start(s32[2]{0:T(128)S(1)} %fusion.8.length_ref) | copy-start | bytes 28
  12.9 25.6 %collective-permute-start.3 = (bf16[2,128,1024]{2,1,0:T(8,128)(2,1)S(1)}, bf16[2,128,1024]{2,1,0:T(8,128)(2,1)}, u32[]{:S(2)}, u32[]{:S(2)}) collective-permute-start(bf16[2,128,1024]{2,1,0:T(8,128)(2,1)S(1)} %broadcast_select_fusion.1), channel_id=1, source_target_pairs={{0,6},{1,7},{2,0},{3,1},{4,2},{5,3},{6,4},{7,5},{8,14},{9,15},{10,... | collective-permute-start | bytes 1572872 | tf_op jit(solution)/shard_map/ppermute | solution.py:136
  15.7 22.8 %collective-permute-start.2 = (bf16[2,128,1024]{2,1,0:T(8,128)(2,1)S(1)}, bf16[2,128,1024]{2,1,0:T(8,128)(2,1)}, u32[]{:S(2)}, u32[]{:S(2)}) collective-permute-start(bf16[2,128,1024]{2,1,0:T(8,128)(2,1)S(1)} %broadcast_select_fusion.1), channel_id=1, source_target_pairs={{0,4},{1,5},{2,6},{3,7},{4,0},{5,1},{6,2},{7,3},{8,12},{9,13},{10,... | collective-permute-start | bytes 1572872 | tf_op jit(solution)/shard_map/ppermute | solution.py:136
  16.5 25.7 %collective-permute-start.1 = (bf16[2,128,1024]{2,1,0:T(8,128)(2,1)S(1)}, bf16[2,128,1024]{2,1,0:T(8,128)(2,1)}, u32[]{:S(2)}, u32[]{:S(2)}) collective-permute-start(bf16[2,128,1024]{2,1,0:T(8,128)(2,1)S(1)} %broadcast_select_fusion.1), channel_id=1, source_target_pairs={{0,2},{1,3},{2,4},{3,5},{4,6},{5,7},{6,0},{7,1},{8,10},{9,11},{10,... | collective-permute-start | bytes 1572872 | tf_op jit(solution)/shard_map/ppermute | solution.py:136
  48.8 2.6 %copy-start.1 = (bf16[4,2,128,1024]{3,2,1,0:T(8,128)(2,1)S(1)}, bf16[4,2,128,1024]{3,2,1,0:T(8,128)(2,1)}, u32[]{:S(2)}) copy-start(bf16[4,2,128,1024]{3,2,1,0:T(8,128)(2,1)} %gather_fusion.1) | copy-start | bytes 6291460
  51.5 1.0 copy-start.5
  54.7 1.4 collective-permute-start.4
  56.9 5.0 %collective-permute-start.7 = (bf16[2,128,128]{2,1,0:T(8,128)(2,1)S(1)}, bf16[2,128,128]{2,1,0:T(8,128)(2,1)S(1)}, u32[]{:S(2)}, u32[]{:S(2)}) collective-permute-start(bf16[2,128,128]{2,1,0:T(8,128)(2,1)S(1)} %get-tuple-element.18), channel_id=1, source_target_pairs={{0,6},{1,7},{2,0},{3,1},{4,2},{5,3},{6,4},{7,5},{8,14},{9,15},{10,... | collective-permute-start | bytes 196616 | tf_op jit(solution)/shard_map/ppermute | solution.py:112
  57.6 5.8 %collective-permute-start.6 = (bf16[2,128,128]{2,1,0:T(8,128)(2,1)S(1)}, bf16[2,128,128]{2,1,0:T(8,128)(2,1)S(1)}, u32[]{:S(2)}, u32[]{:S(2)}) collective-permute-start(bf16[2,128,128]{2,1,0:T(8,128)(2,1)S(1)} %get-tuple-element.16), channel_id=1, source_target_pairs={{0,4},{1,5},{2,6},{3,7},{4,0},{5,1},{6,2},{7,3},{8,12},{9,13},{10,... | collective-permute-start | bytes 196616 | tf_op jit(solution)/shard_map/ppermute | solution.py:112
  58.4 6.0 %collective-permute-start.5 = (bf16[2,128,128]{2,1,0:T(8,128)(2,1)S(1)}, bf16[2,128,128]{2,1,0:T(8,128)(2,1)S(1)}, u32[]{:S(2)}, u32[]{:S(2)}) collective-permute-start(bf16[2,128,128]{2,1,0:T(8,128)(2,1)S(1)} %get-tuple-element.17), channel_id=1, source_target_pairs={{0,2},{1,3},{2,4},{3,5},{4,6},{5,7},{6,0},{7,1},{8,10},{9,11},{10,... | collective-permute-start | bytes 196616 | tf_op jit(solution)/shard_map/ppermute | solution.py:112

commit v9 on v7

--- a/solution.py
+++ b/solution.py
@@ -32,11 +32,7 @@
 
     span = group * BLK
 
-    @pl.when(step * span < length)
-    def _():
-        kv = jnp.concatenate([ref[0] for ref in pool_refs], axis=0)
-        positions = step * span + lax.broadcasted_iota(jnp.int32, (span, 1), 0)
-        kv = jnp.where(positions < length, kv, jnp.zeros_like(kv))
+    def accumulate(kv):
         for h in range(heads):
             lanes = slice(h * 2 * DH, (h + 1) * 2 * DH)
             pair = kv[:, lanes]
@@ -46,6 +42,16 @@
             )
             weights = (half + half * jnp.tanh(half)).astype(jnp.bfloat16)
             acc_ref[:, lanes] += jnp.dot(weights, pair, preferred_element_type=jnp.float32)
+
+    @pl.when((step + 1) * span <= length)
+    def _():
+        accumulate(jnp.concatenate([ref[0] for ref in pool_refs], axis=0))
+
+    @pl.when(jnp.logical_and(step * span < length, length < (step + 1) * span))
+    def _():
+        kv = jnp.concatenate([ref[0] for ref in pool_refs], axis=0)
+        positions = step * span + lax.broadcasted_iota(jnp.int32, (span, 1), 0)
+        accumulate(jnp.where(positions < length, kv, jnp.zeros_like(kv)))
 
     @pl.when(step == pl.num_programs(1) - 1)
     def _():

time: 178 us -> 180 us (1.011); the launches traced: 177 us -> 177 us
  no operation moved by 1% of the time
where the time goes in v9:
time: 180 us; the launch traced here: 177 us
  waiting for transfers between devices  115 us (64%)
  starting transfers between devices  17.4 us (10%)
  blocking collectives  11.9 us (7%)
  local copies, waits for them, and re-layouts  10.6 us (6%)
  Pallas kernels  10.4 us (6%)
  other arithmetic  8.21 us (5%)
  matrix products  2.45 us (1%)
    all_to_all x1, waiting for transfers between devices, shards(): lax.all_to_all(kv_cache, 'req', split_axis=1, concat_axis=0, tiled=True)  87.5 us
    ppermute x3, waiting for transfers between devices, gather_rows(): received.append(lax.ppermute(pair, axis, perm=pairs))  24 us
    all_to_all x1, blocking collectives, shards(): lax.all_to_all(attn, 'head', split_axis=0, concat_axis=1, tiled=True)  11.9 us
    pallas_call x1, Pallas kernels, attention(): pl.pallas_call(kernel, grid_spec=grid_spec, out_shape=jax.ShapeDtypeStruc...  10.4 us
    all_to_all x1, starting transfers between devices, shards(): lax.all_to_all(kv_cache, 'req', split_axis=1, concat_axis=0, tiled=True)  10.4 us
    ppermute x3, starting transfers between devices, gather_rows(): received.append(lax.ppermute(pair, axis, perm=pairs))  4.52 us
    gather x1, local copies, waits for them, and re-layouts, gather_rows(): ordered = jnp.take(stacked, sources, axis=0)  3.64 us
  transfers between devices with their start and end apart: 9, of which 8 were waited for; matrix products, arithmetic and copies ran while one was open for 11% of the time, Pallas kernels for 0%

profile of v9, /device:TPU:112, one launch (start us, length us, event | category | flops | bytes accessed | tf_op | source)
XLA Modules:
  0.0 176.7 jit_solution(7609288327310090492)
XLA Ops:
  0.0 10.4 %all-to-all-start = ((bf16[1,32,3,128,256]{4,3,2,0,1:T(8,128)(2,1)}), bf16[1,32,3,128,256]{4,3,2,0,1:T(8,128)(2,1)}, u32[]{:S(2)}, u32[]{:S(2)}) async-start(bf16[1,32,3,128,256]{4,3,2,0,1:T(8,128)(2,1)} %bitcast.70), calls=%async_computation | async-start | bytes 12582912 | tf_op jit(solution)/shard_map/all_to_all | solution.py:151
  10.5 0.1 collective-permute-start
  10.7 0.1 reduce_window_sum.11
  10.9 0.2 fusion.8.length_ref
  11.1 0.2 select_reduce_fusion
  11.4 0.7 collective-permute-done
  12.1 0.6 gather_fusion
  12.7 0.1 broadcast_select_fusion.1
  12.9 2.8 %collective-permute-start.3 = (bf16[2,128,1024]{2,1,0:T(8,128)(2,1)S(1)}, bf16[2,128,1024]{2,1,0:T(8,128)(2,1)}, u32[]{:S(2)}, u32[]{:S(2)}) collective-permute-start(bf16[2,128,1024]{2,1,0:T(8,128)(2,1)S(1)} %broadcast_select_fusion.1), channel_id=1, source_target_pairs={{0,6},{1,7},{2,0},{3,1},{4,2},{5,3},{6,4},{7,5},{8,14},{9,15},{10,... | collective-permute-start | bytes 1572872 | tf_op jit(solution)/shard_map/ppermute | solution.py:142
  15.7 0.8 collective-permute-start.2
  16.5 0.9 collective-permute-start.1
  18.1 0.1 bitcast_select_fusion.1
  18.2 20.2 %collective-permute-done.3 = bf16[2,128,1024]{2,1,0:T(8,128)(2,1)} collective-permute-done((bf16[2,128,1024]{2,1,0:T(8,128)(2,1)S(1)}, bf16[2,128,1024]{2,1,0:T(8,128)(2,1)}, u32[]{:S(2)}, u32[]{:S(2)}) %collective-permute-start.3) | collective-permute-done | bytes 524320 | tf_op jit(solution)/shard_map/ppermute | solution.py:142
  38.4 3.8 %collective-permute-done.1 = bf16[2,128,1024]{2,1,0:T(8,128)(2,1)} collective-permute-done((bf16[2,128,1024]{2,1,0:T(8,128)(2,1)S(1)}, bf16[2,128,1024]{2,1,0:T(8,128)(2,1)}, u32[]{:S(2)}, u32[]{:S(2)}) %collective-permute-start.1) | collective-permute-done | bytes 524320 | tf_op jit(solution)/shard_map/ppermute | solution.py:142
  42.2 3.0 %pad_maximum_fusion = bf16[4,2,128,1024]{3,2,1,0:T(8,128)(2,1)} fusion(bf16[1,2,128,1024]{3,2,1,0:T(8,128)(2,1)} %bitcast.11, bf16[1,2,128,1024]{3,2,1,0:T(8,128)(2,1)} %bitcast.10, bf16[1,2,128,1024]{3,2,1,0:T(8,128)(2,1)} %bitcast.9, bf16[1,2,128,1024]{3,2,1,0:T(8,128)(2,1)S(1)} %bitcast_select_fusion.1), kind=kLoop, calls=%fused_computation.10 | loop fusion | flops 3145728 | bytes 4194304 | tf_op jit(solution)/shard_map/stack | solution.py:143
  45.2 3.6 %gather_fusion.1 = bf16[4,2,128,1024]{3,2,1,0:T(8,128)(2,1)} fusion(bf16[4,2,128,1024]{3,2,1,0:T(8,128)(2,1)} %pad_maximum_fusion, s32[1024]{0:T(1024)S(1)} %pad_clamp_fusion), kind=kCustom, calls=%fused_computation.1 | custom fusion | bytes 4194320 | tf_op jit(solution)/shard_map/jit(_take)/gather | solution.py:145
  48.8 2.6 %convert_reduce_fusion = (f32[4,2,128]{2,1,0:T(2,128)S(1)}, f32[4,2,128]{2,1,0:T(2,128)S(1)}) fusion(bf16[4,2,128,1024]{3,2,1,0:T(8,128)(2,1)} %gather_fusion.1, pred[4]{0:T(512)(128)(4,1)S(1)} %compare_and_fusion.1), kind=kLoop, calls=%fused_computation.6 | loop fusion | flops 5240832 | bytes 2105348 | tf_op jit(solution)/shard_map/reduce_sum | solution.py:17
  51.5 0.4 bitcast_select_fusion
  51.9 0.6 copy-done.5
  52.5 1.3 multiply_convert_fusion.2
  53.8 0.2 convert_element_type.47
  54.0 0.5 constant_dynamic-slice_fusion.1
  54.6 0.2 copy.27
  54.7 0.1 collective-permute-start.4
  54.8 0.9 gather_fusion.4
  55.7 0.2 copy.33
  55.9 0.3 collective-permute-done.4
  56.2 0.6 gather_fusion.2
  56.8 0.1 broadcast_select_fusion.2
  56.9 0.7 collective-permute-start.7
  57.6 0.8 collective-permute-start.6
  58.4 0.8 collective-permute-start.5
  59.2 0.6 and_select_fusion.2.index_ref
  59.8 0.4 copy.36
  60.2 0.5 concatenate.24
  60.7 0.9 copy.38
  61.6 0.3 collective-permute-done.7
  61.9 1.5 collective-permute-done.6
  63.4 1.0 collective-permute-done.5
  64.5 0.6 gather_fusion.3
  65.1 0.1 select_bitcast_fusion
  65.2 0.2 copy.29
  65.4 87.5 %all-to-all-done = bf16[1,32,3,128,256]{4,3,2,0,1:T(8,128)(2,1)} async-done(((bf16[1,32,3,128,256]{4,3,2,0,1:T(8,128)(2,1)}), bf16[1,32,3,128,256]{4,3,2,0,1:T(8,128)(2,1)}, u32[]{:S(2)}, u32[]{:S(2)}) %all-to-all-start) | async-done | bytes 6291488 | tf_op jit(solution)/shard_map/all_to_all | solution.py:151
  152.9 10.4 %shard_map.73 = bf16[8,128,128]{2,1,0:T(8,128)(2,1)} custom-call(s32[64]{0:T(128)} %and_select_fusion.2.index_ref, s32[2]{0:T(128)} %copy-done.4, bf16[1024,256]{1,0:T(8,128)(2,1)} %bitcast.71, ...), custom_call_target="tpu_custom_call" | custom-call | tf_op jit(solution)/shard_map/pallas_call | solution.py:87
  163.4 11.9 %all_to_all.9 = bf16[8,128,128]{1,2,0:T(8,128)(2,1)S(1)} all-to-all(bf16[8,128,128]{1,2,0:T(8,128)(2,1)} %bitcast.74), channel_id=1, replica_groups=mesh['req'=32,'head'=8] {'head'}, dimensions={0} | all-to-all | bytes 524288 | tf_op jit(solution)/shard_map/all_to_all | solution.py:187
  175.2 0.2 convert_reduce_fusion.1
  175.4 0.1 fusion.6
  175.5 1.2 convolution_convert_fusion
  (44 shorter events, 1.2 us)
Async XLA Ops:
  0.0 175.5 %copy-start = (bf16[1024,1024]{1,0:T(8,128)(2,1)S(1)}, bf16[1024,1024]{1,0:T(8,128)(2,1)}, u32[]{:S(2)}) copy-start(bf16[1024,1024]{1,0:T(8,128)(2,1)} %param.9) | copy-start | bytes 6291460
  0.0 10.5 %copy-start.2 = (bf16[128,1024]{1,0:T(8,128)(2,1)S(1)}, bf16[128,1024]{1,0:T(8,128)(2,1)}, u32[]{:S(2)}) copy-start(bf16[128,1024]{1,0:T(8,128)(2,1)} %param.7) | copy-start | bytes 786436
  0.0 10.6 %copy-start.3 = (s32[64,1]{0,1:T(1,128)S(1)}, s32[64,1]{0,1:T(1,128)}, u32[]{:S(2)}) copy-start(s32[64,1]{0,1:T(1,128)} %param.13) | copy-start | bytes 772
  0.0 10.9 %copy-start.6 = (s32[64]{0:T(128)S(1)}, s32[64]{0:T(128)}, u32[]{:S(2)}) copy-start(s32[64]{0:T(128)} %param.12) | copy-start | bytes 772
  0.0 10.9 %copy-start.7 = (s32[2]{0:T(128)S(1)}, s32[2]{0:T(128)}, u32[]{:S(2)}) copy-start(s32[2]{0:T(128)} %param.11) | copy-start | bytes 28
  0.0 152.9 %all-to-all-start = ((bf16[1,32,3,128,256]{4,3,2,0,1:T(8,128)(2,1)}), bf16[1,32,3,128,256]{4,3,2,0,1:T(8,128)(2,1)}, u32[]{:S(2)}, u32[]{:S(2)}) async-start(bf16[1,32,3,128,256]{4,3,2,0,1:T(8,128)(2,1)} %bitcast.70), calls=%async_computation | async-start | bytes 12582912 | tf_op jit(solution)/shard_map/all_to_all | solution.py:151
  10.5 1.6 collective-permute-start
  11.1 7.1 %copy-start.4 = (s32[2]{0:T(128)}, s32[2]{0:T(128)S(1)}, u32[]{:S(2)}) copy-start(s32[2]{0:T(128)S(1)} %fusion.8.length_ref) | copy-start | bytes 28
  12.9 25.6 %collective-permute-start.3 = (bf16[2,128,1024]{2,1,0:T(8,128)(2,1)S(1)}, bf16[2,128,1024]{2,1,0:T(8,128)(2,1)}, u32[]{:S(2)}, u32[]{:S(2)}) collective-permute-start(bf16[2,128,1024]{2,1,0:T(8,128)(2,1)S(1)} %broadcast_select_fusion.1), channel_id=1, source_target_pairs={{0,6},{1,7},{2,0},{3,1},{4,2},{5,3},{6,4},{7,5},{8,14},{9,15},{10,... | collective-permute-start | bytes 1572872 | tf_op jit(solution)/shard_map/ppermute | solution.py:142
  15.7 22.8 %collective-permute-start.2 = (bf16[2,128,1024]{2,1,0:T(8,128)(2,1)S(1)}, bf16[2,128,1024]{2,1,0:T(8,128)(2,1)}, u32[]{:S(2)}, u32[]{:S(2)}) collective-permute-start(bf16[2,128,1024]{2,1,0:T(8,128)(2,1)S(1)} %broadcast_select_fusion.1), channel_id=1, source_target_pairs={{0,4},{1,5},{2,6},{3,7},{4,0},{5,1},{6,2},{7,3},{8,12},{9,13},{10,... | collective-permute-start | bytes 1572872 | tf_op jit(solution)/shard_map/ppermute | solution.py:142
  16.5 25.7 %collective-permute-start.1 = (bf16[2,128,1024]{2,1,0:T(8,128)(2,1)S(1)}, bf16[2,128,1024]{2,1,0:T(8,128)(2,1)}, u32[]{:S(2)}, u32[]{:S(2)}) collective-permute-start(bf16[2,128,1024]{2,1,0:T(8,128)(2,1)S(1)} %broadcast_select_fusion.1), channel_id=1, source_target_pairs={{0,2},{1,3},{2,4},{3,5},{4,6},{5,7},{6,0},{7,1},{8,10},{9,11},{10,... | collective-permute-start | bytes 1572872 | tf_op jit(solution)/shard_map/ppermute | solution.py:142
  48.8 2.6 %copy-start.1 = (bf16[4,2,128,1024]{3,2,1,0:T(8,128)(2,1)S(1)}, bf16[4,2,128,1024]{3,2,1,0:T(8,128)(2,1)}, u32[]{:S(2)}) copy-start(bf16[4,2,128,1024]{3,2,1,0:T(8,128)(2,1)} %gather_fusion.1) | copy-start | bytes 6291460
  51.5 1.0 copy-start.5
  54.7 1.4 collective-permute-start.4
  56.9 5.0 %collective-permute-start.7 = (bf16[2,128,128]{2,1,0:T(8,128)(2,1)S(1)}, bf16[2,128,128]{2,1,0:T(8,128)(2,1)S(1)}, u32[]{:S(2)}, u32[]{:S(2)}) collective-permute-start(bf16[2,128,128]{2,1,0:T(8,128)(2,1)S(1)} %get-tuple-element.18), channel_id=1, source_target_pairs={{0,6},{1,7},{2,0},{3,1},{4,2},{5,3},{6,4},{7,5},{8,14},{9,15},{10,... | collective-permute-start | bytes 196616 | tf_op jit(solution)/shard_map/ppermute | solution.py:118
  57.6 5.8 %collective-permute-start.6 = (bf16[2,128,128]{2,1,0:T(8,128)(2,1)S(1)}, bf16[2,128,128]{2,1,0:T(8,128)(2,1)S(1)}, u32[]{:S(2)}, u32[]{:S(2)}) collective-permute-start(bf16[2,128,128]{2,1,0:T(8,128)(2,1)S(1)} %get-tuple-element.16), channel_id=1, source_target_pairs={{0,4},{1,5},{2,6},{3,7},{4,0},{5,1},{6,2},{7,3},{8,12},{9,13},{10,... | collective-permute-start | bytes 196616 | tf_op jit(solution)/shard_map/ppermute | solution.py:118
  58.4 6.0 %collective-permute-start.5 = (bf16[2,128,128]{2,1,0:T(8,128)(2,1)S(1)}, bf16[2,128,128]{2,1,0:T(8,128)(2,1)S(1)}, u32[]{:S(2)}, u32[]{:S(2)}) collective-permute-start(bf16[2,128,128]{2,1,0:T(8,128)(2,1)S(1)} %get-tuple-element.17), channel_id=1, source_target_pairs={{0,2},{1,3},{2,4},{3,5},{4,6},{5,7},{6,0},{7,1},{8,10},{9,11},{10,... | collective-permute-start | bytes 196616 | tf_op jit(solution)/shard_map/ppermute | solution.py:118
